TPU v7x, 32 devices: a whole 2x2x4 slice. The times are simulated.
32 devices in a mesh: gx: 2 (over core), ga: 4 (over y, x), gz: 4 (over z).
Axes of the slice: x: 2, y: 2, z: 4, core: 2. Of those that a mesh axis runs over, the one named last changes fastest.
Arguments:
- right_side: float32 [32, 64, 512], P('gx', 'ga', 'gz'), may hold values from -15 to 15
- diagonal: float32 [32, 64, 512], P('gx', 'ga', 'gz'), may hold values from 0.25 to 2
- basis_tables: float32 [3, 12, 12], replicated, may hold values from -1.75 to 1.75
- eigenvalues: float32 [3, 12], replicated, may hold values from 0.3 to 3
- coarse_blocks: float32 [2, 4, 4, 2, 64, 64], P('gx', 'ga', 'gz'), may hold values from -1 to 1
- coarse_columns: int32 [2, 4, 4, 2], P('gx', 'ga', 'gz'), may hold values from 0 to 15
Outputs:
- solution: float32 [32, 64, 512], P('gx', 'ga', 'gz')
- residual: float32 [32, 64, 512], P('gx', 'ga', 'gz')
All inputs are finite; a program needn't handle non-finite values.
Results may differ from a plain program's by a relative error of at most 0.0003.
Values sent between devices are 32-bit elements; how exact they have to be, the bound alone decides.
No kernel may reach another device: no remote copies, remote signals or barrier semaphores. Data moves between devices by JAX's collectives and lax.ppermute only.
A program may use at most 64 MiB of HBM per device.

v0:
```python
import jax
import jax.numpy as jnp
from jax import lax
from jax.sharding import PartitionSpec as P

PTS = 8
RIM = 2
WIDE = 12
CYCLES = 2


PRECISE = lax.Precision.HIGHEST


def padded_2(value, sides, width):
    for axis, dim in sides:
        size, length = (lax.axis_size(axis), value.shape[dim])
        last = lax.slice_in_dim(value, length - width, length, axis=dim)
        leading = lax.slice_in_dim(value, 0, width, axis=dim)
        if size == 2:
            first = lax.axis_index(axis) == 0
            got = lax.ppermute(jnp.where(first, last, leading), axis, [(0, 1), (1, 0)])
            zero = jnp.zeros_like(got)
            before = jnp.where(first, zero, got)
            after = jnp.where(first, got, zero)
        else:
            up = [(i, (i + 1) % size) for i in range(size - 1)]
            down = [(j, i) for i, j in up]
            before = lax.ppermute(last, axis, up)
            after = lax.ppermute(leading, axis, down)
        value = jnp.concatenate([before, value, after], axis=dim)
    return value


SIDES = (("gx", 0), ("ga", 1), ("gz", 2))


def operate_rim(zed, diagonal, inside):
    centre = zed[1:-1, 1:-1, 1:-1]
    beside = zed[2:, 1:-1, 1:-1] + zed[:-2, 1:-1, 1:-1]
    beside = beside + zed[1:-1, 2:, 1:-1] + zed[1:-1, :-2, 1:-1]
    beside = beside + zed[1:-1, 1:-1, 2:] + zed[1:-1, 1:-1, :-2]
    return ((6.0 + diagonal) * centre - beside) * inside


def inside_grid(shape, width):
    result = None
    for axis, dim in SIDES:
        length = shape[dim]
        place = lax.axis_index(axis) * length - width + jnp.arange(length + 2 * width, dtype=jnp.int32)
        line = ((place >= 0) & (place < lax.axis_size(axis) * length)).astype(jnp.float32)
        view = [1, 1, 1]
        view[dim] = length + 2 * width
        line = line.reshape(view)
        result = line if result is None else result * line
    return result


def interior(value, width):
    return value[width:-width, width:-width, width:-width]


def forward_table(count, basis):
    row_index = jnp.arange(PTS * count + 2 * RIM, dtype=jnp.int32)
    element = jnp.arange(count, dtype=jnp.int32)
    offset = jnp.arange(WIDE, dtype=jnp.int32)
    select = (
        row_index[:, None, None] == PTS * element[None, :, None] + offset[None, None, :]
    ).astype(jnp.float32)
    table = jnp.einsum("rcj,jm->rcm", select, basis, precision=PRECISE)
    return table.reshape(PTS * count + 2 * RIM, count * WIDE)


def backward_table(count, basis):
    same = jnp.eye(count, dtype=jnp.float32)
    table = jnp.einsum("cd,im->cmdi", same, basis[RIM : RIM + PTS], precision=PRECISE)
    return table.reshape(count * WIDE, count * PTS)


def schwarz_part(padded, basis_tables, eigenvalues):
    count_x = (padded.shape[0] - 2 * RIM) // PTS
    count_y = (padded.shape[1] - 2 * RIM) // PTS
    count_z = (padded.shape[2] - 2 * RIM) // PTS
    spectral = jnp.einsum(
        "pqr,rc->pqc", padded, forward_table(count_z, basis_tables[2]), precision=PRECISE
    )
    spectral = jnp.einsum(
        "pqc,pa->aqc", spectral, forward_table(count_x, basis_tables[0]), precision=PRECISE
    )
    spectral = jnp.einsum(
        "aqc,qb->abc", spectral, forward_table(count_y, basis_tables[1]), precision=PRECISE
    )
    denominator = (
        jnp.tile(eigenvalues[0], count_x)[:, None, None]
        + jnp.tile(eigenvalues[1], count_y)[None, :, None]
    )
    denominator = denominator + jnp.tile(eigenvalues[2], count_z)[None, None, :]
    spectral = spectral / denominator
    local_part = jnp.einsum(
        "abc,cr->abr", spectral, backward_table(count_z, basis_tables[2]), precision=PRECISE
    )
    local_part = jnp.einsum(
        "abr,ap->pbr", local_part, backward_table(count_x, basis_tables[0]), precision=PRECISE
    )
    local_part = jnp.einsum(
        "pbr,bq->pqr", local_part, backward_table(count_y, basis_tables[1]), precision=PRECISE
    )
    return local_part


def coarse_terms(field, blocks, selector):
    count_x = field.shape[0] // PTS
    count_y = field.shape[1] // PTS
    count_z = field.shape[2] // PTS
    cells = count_x * count_y * count_z
    means = jnp.mean(field.reshape(count_x, PTS, count_y, PTS, count_z, PTS), axis=(1, 3, 5))
    restricted = means.reshape(cells)
    terms = jnp.einsum("kpq,p->kq", blocks, restricted, precision=PRECISE)
    return jnp.einsum("kj,kq->jq", selector, terms, precision=PRECISE)


def element_table(blocks, columns, shape):
    count = blocks.shape[0]
    grid = (shape[0] // PTS, shape[1] // PTS, shape[2] // PTS)
    rows = jnp.transpose(blocks, (1, 0, 2)).reshape(grid + (count * blocks.shape[2],))
    cols = jnp.broadcast_to(columns.astype(jnp.float32), grid + (count,))
    return jnp.concatenate([rows, cols], axis=-1)


def coarse_rim(wholes, table, count, group):
    lo, whole, hi = wholes
    grid = table.shape[:3]
    width = (table.shape[3] - count) // count
    rows = table[..., : count * width].reshape(grid + (count, width))
    cols = table[..., count * width :]
    onehot = (cols[..., None] == jnp.arange(group, dtype=jnp.float32)).astype(jnp.float32)
    stacked = jnp.stack([lo] + [whole] * (grid[0] - 2) + [hi])
    picked = jnp.einsum("abckg,agq->abckq", onehot, stacked, precision=PRECISE)
    return jnp.sum(rows * picked, axis=(3, 4))


def spread_rim(values, width, shape):
    def table(length, count):
        point = jnp.arange(length + 2 * width, dtype=jnp.int32) - width + PTS
        element = jnp.arange(count, dtype=jnp.int32)
        return (point[:, None] // PTS == element[None, :]).astype(jnp.float32)

    grid = values.shape
    out = jnp.einsum("abc,rc->abr", values, table(shape[2], grid[2]), precision=PRECISE)
    out = jnp.einsum("abr,pa->pbr", out, table(shape[0], grid[0]), precision=PRECISE)
    return jnp.einsum("pbr,qb->pqr", out, table(shape[1], grid[1]), precision=PRECISE)


ALL = ("gx", "ga", "gz")


def butterfly(value, axes):
    for axis in axes:
        size = lax.axis_size(axis)
        if size & (size - 1):
            value = lax.psum(value, axis)
            continue
        step = 1
        while step < size:
            value = value + lax.ppermute(value, axis, [(i, i ^ step) for i in range(size)])
            step *= 2
    return value


def reduce_scalars(scalars):
    total = butterfly(lax.optimization_barrier(jnp.stack(scalars)), ALL)
    return [total[i] for i in range(len(scalars))]


def reduce_coarse(buffer, scalars):
    count = len(scalars)
    payload = lax.optimization_barrier(jnp.concatenate([buffer.reshape(-1), jnp.stack(scalars)]))
    payload = butterfly(payload, ("ga", "gz"))
    size = payload.shape[0] - count
    whole = payload[:size].reshape(buffer.shape)
    if lax.axis_size("gx") == 2:
        got = lax.ppermute(payload, "gx", [(0, 1), (1, 0)])
        total = payload[size:] + got[size:]
        other = got[:size].reshape(buffer.shape)
        first = lax.axis_index("gx") == 0
        zero = jnp.zeros_like(other)
        lo, hi = jnp.where(first, zero, other), jnp.where(first, other, zero)
    else:
        total = butterfly(payload[size:], ("gx",))
        gx = lax.axis_size("gx")
        up = [(i, i + 1) for i in range(gx - 1)]
        lo = lax.ppermute(whole, "gx", up)
        hi = lax.ppermute(whole, "gx", [(j, i) for i, j in up])
    return (lo, whole, hi), [total[i] for i in range(count)]


def body(right_side, diagonal, basis_tables, eigenvalues, coarse_blocks, coarse_columns):
    blocks = coarse_blocks.reshape(coarse_blocks.shape[3:])
    columns = coarse_columns.reshape(coarse_columns.shape[3])
    count = blocks.shape[0]
    group = lax.axis_size(("ga", "gz"))
    selector = (columns[:, None] == jnp.arange(group, dtype=jnp.int32)[None, :]).astype(jnp.float32)
    shape = right_side.shape
    stacked = tuple((axis, dim + 1) for axis, dim in SIDES)
    wide_pair = padded_2(jnp.stack([diagonal, right_side]), stacked, RIM)
    wide_diagonal, wide_residual = wide_pair[0], wide_pair[1]
    inside = inside_grid(shape, RIM)
    table = padded_2(element_table(blocks, columns, shape), SIDES, 1)

    def precondition_rim(wide_field, field):
        local = schwarz_part(wide_field, basis_tables, eigenvalues)
        return padded_2(local, SIDES, RIM + 1), coarse_terms(field, blocks, selector)

    def coarse_on_rim(wholes):
        return spread_rim(coarse_rim(wholes, table, count, group), RIM + 1, shape)

    solution = jnp.zeros_like(right_side)
    for restart in range(CYCLES):
        residual = interior(wide_residual, RIM)
        wide_local, terms = precondition_rim(wide_residual, residual)
        wholes, (square,) = reduce_coarse(terms, [jnp.sum(residual * residual)])
        initial_norm = jnp.sqrt(square)
        first_vector = residual / initial_norm
        wide_zed = (wide_local + coarse_on_rim(wholes)) / initial_norm
        first_zed = interior(wide_zed, RIM + 1)
        wide_first = operate_rim(wide_zed, wide_diagonal, inside)
        first_image = interior(wide_first, RIM)
        wide_local, terms = precondition_rim(wide_first, first_image)
        wholes, (first_proj, image_square) = reduce_coarse(
            terms, [jnp.sum(first_vector * first_image), jnp.sum(first_image * first_image)]
        )
        first_len = jnp.sqrt(image_square - first_proj * first_proj)
        second_vector = (first_image - first_proj * first_vector) / first_len
        wide_second_zed = (wide_local + coarse_on_rim(wholes) - first_proj * wide_zed) / first_len
        second_zed = interior(wide_second_zed, RIM + 1)
        wide_second = operate_rim(wide_second_zed, wide_diagonal, inside)
        second_image = interior(wide_second, RIM)
        upper_proj, lower_proj, second_square = reduce_scalars(
            [
                jnp.sum(first_vector * second_image),
                jnp.sum(second_vector * second_image),
                jnp.sum(second_image * second_image),
            ]
        )
        second_len = jnp.sqrt(second_square - upper_proj * upper_proj - lower_proj * lower_proj)
        gram_first = first_proj * first_proj + first_len * first_len
        gram_cross = first_proj * upper_proj + first_len * lower_proj
        gram_second = upper_proj * upper_proj + lower_proj * lower_proj + second_len * second_len
        target_first = initial_norm * first_proj
        target_second = initial_norm * upper_proj
        determinant = gram_first * gram_second - gram_cross * gram_cross
        weight_first = (gram_second * target_first - gram_cross * target_second) / determinant
        weight_second = (gram_first * target_second - gram_cross * target_first) / determinant
        solution = solution + weight_first * first_zed + weight_second * second_zed
        wide_residual = wide_residual - weight_first * wide_first - weight_second * wide_second
    return (solution, interior(wide_residual, RIM))


def solution(mesh):
    in_specs = (
        P("gx", "ga", "gz"),
        P("gx", "ga", "gz"),
        P(),
        P(),
        P("gx", "ga", "gz", None, None, None),
        P("gx", "ga", "gz", None),
    )
    out_specs = (P("gx", "ga", "gz"), P("gx", "ga", "gz"))
    return jax.shard_map(body, mesh=mesh, in_specs=in_specs, out_specs=out_specs, check_vma=False)
```

profile of v0, /device:TPU:0, one launch (start us, length us, event | category | flops | bytes accessed | tf_op | source)
XLA Modules:
  0.0 309.2 jit_solution(6363749661422097166)
XLA Ops:
  9.8 4.8 %collective-permute-start.16 = (f32[4,1,16,130]{3,2,1,0:T(8,128)S(1)}, f32[4,1,16,130]{3,2,1,0:T(8,128)S(1)}, u32[]{:S(2)}, u32[]{:S(2)}) collective-permute-start(f32[4,1,16,130]{3,2,1,0:T(8,128)S(1)} %get-tuple-element.40), channel_id=1, source_target_pairs={{0,4},{4,8},{8,12},{1,5},{5,9},{9,13},{2,6},{6,10},{10,14},{3,7},{... | collective-permute-start | bytes 99848 | tf_op jit(solution)/shard_map/ppermute | solution.py:29
  16.1 4.5 %collective-permute-start.1 = (f32[2,20,2,128]{3,2,1,0:T(2,128)S(1)}, f32[2,20,2,128]{3,2,1,0:T(2,128)S(1)}, u32[]{:S(2)}, u32[]{:S(2)}) collective-permute-start(f32[2,20,2,128]{3,2,1,0:T(2,128)S(1)} %get-tuple-element.20), channel_id=1, source_target_pairs={{0,4},{4,8},{8,12},{1,5},{5,9},{9,13},{2,6},{6,10},{10,14},{3,7},{... | collective-permute-start | bytes 122888 | tf_op jit(solution)/shard_map/ppermute | solution.py:29
  22.0 3.5 %collective-permute-start.18 = (f32[4,4,1,130]{3,2,1,0:T(1,128)S(1)}, f32[4,4,1,130]{3,2,1,0:T(1,128)S(1)}, u32[]{:S(2)}, u32[]{:S(2)}) collective-permute-start(f32[4,4,1,130]{3,2,1,0:T(1,128)S(1)} %get-tuple-element.30), channel_id=1, source_target_pairs={{0,1},{1,2},{2,3},{4,5},{5,6},{6,7},{8,9},{9,10},{10,11},{12,13},{... | collective-permute-start | bytes 24968 | tf_op jit(solution)/shard_map/ppermute | solution.py:29
  28.1 4.5 %collective-permute-start.3 = (f32[2,20,20,2]{3,2,1,0:T(8,128)}, f32[2,20,20,2]{3,2,1,0:T(8,128)S(1)}, u32[]{:S(2)}, u32[]{:S(2)}) collective-permute-start(f32[2,20,20,2]{3,2,1,0:T(8,128)} %get-tuple-element.18), channel_id=1, source_target_pairs={{0,1},{1,2},{2,3},{4,5},{5,6},{6,7},{8,9},{9,10},{10,11},{12,13},{... | collective-permute-start | bytes 19208 | tf_op jit(solution)/shard_map/ppermute | solution.py:29
  34.4 7.7 %collective-permute-done.3 = f32[2,20,20,2]{3,2,1,0:T(8,128)S(1)} collective-permute-done((f32[2,20,20,2]{3,2,1,0:T(8,128)}, f32[2,20,20,2]{3,2,1,0:T(8,128)S(1)}, u32[]{:S(2)}, u32[]{:S(2)}) %collective-permute-start.3) | collective-permute-done | bytes 6432 | tf_op jit(solution)/shard_map/ppermute | solution.py:29
  42.1 4.0 %collective-permute-done.4 = f32[2,20,20,2]{3,2,1,0:T(8,128)S(1)} collective-permute-done((f32[2,20,20,2]{3,2,1,0:T(8,128)}, f32[2,20,20,2]{3,2,1,0:T(8,128)S(1)}, u32[]{:S(2)}, u32[]{:S(2)}) %collective-permute-start.4) | collective-permute-done | bytes 6432 | tf_op jit(solution)/shard_map/ppermute | solution.py:30
  77.3 4.9 %collective-permute-done.12 = f32[22,3,128]{2,1,0:T(4,128)S(1)} collective-permute-done((f32[22,3,128]{2,1,0:T(4,128)S(1)}, f32[22,3,128]{2,1,0:T(4,128)S(1)}, u32[]{:S(2)}, u32[]{:S(2)}) %collective-permute-start.12) | collective-permute-done | bytes 33824 | tf_op jit(solution)/shard_map/ppermute | solution.py:30
  82.3 3.5 %collective-permute-start.13 = (f32[22,22,3]{2,1,0:T(8,128)S(1)}, f32[22,22,3]{2,1,0:T(8,128)S(1)}, u32[]{:S(2)}, u32[]{:S(2)}) collective-permute-start(f32[22,22,3]{2,1,0:T(8,128)S(1)} %get-tuple-element.28), channel_id=1, source_target_pairs={{0,1},{1,2},{2,3},{4,5},{5,6},{6,7},{8,9},{9,10},{10,11},{12,13},{... | collective-permute-start | bytes 17432 | tf_op jit(solution)/shard_map/ppermute | solution.py:29
  90.7 4.1 %collective-permute-done.14 = f32[22,22,3]{2,1,0:T(8,128)S(1)} collective-permute-done((f32[22,22,3]{2,1,0:T(8,128)S(1)}, f32[22,22,3]{2,1,0:T(8,128)S(1)}, u32[]{:S(2)}, u32[]{:S(2)}) %collective-permute-start.14) | collective-permute-done | bytes 5840 | tf_op jit(solution)/shard_map/ppermute | solution.py:30
  123.2 3.9 %collective-permute-start.21 = (f32[22,3,128]{2,1,0:T(4,128)S(1)}, f32[22,3,128]{2,1,0:T(4,128)S(1)}, u32[]{:S(2)}, u32[]{:S(2)}) collective-permute-start(f32[22,3,128]{2,1,0:T(4,128)S(1)} %get-tuple-element.36), channel_id=1, source_target_pairs={{0,4},{4,8},{8,12},{1,5},{5,9},{9,13},{2,6},{6,10},{10,14},{3,7},{... | collective-permute-start | bytes 101384 | tf_op jit(solution)/shard_map/ppermute | solution.py:29
  128.8 4.2 %collective-permute-done.22 = f32[22,3,128]{2,1,0:T(4,128)S(1)} collective-permute-done((f32[22,3,128]{2,1,0:T(4,128)S(1)}, f32[22,3,128]{2,1,0:T(4,128)S(1)}, u32[]{:S(2)}, u32[]{:S(2)}) %collective-permute-start.22) | collective-permute-done | bytes 33824 | tf_op jit(solution)/shard_map/ppermute | solution.py:30
  134.6 3.5 %collective-permute-start.23 = (f32[22,22,3]{2,1,0:T(8,128)}, f32[22,22,3]{2,1,0:T(8,128)S(1)}, u32[]{:S(2)}, u32[]{:S(2)}) collective-permute-start(f32[22,22,3]{2,1,0:T(8,128)} %get-tuple-element.26), channel_id=1, source_target_pairs={{0,1},{1,2},{2,3},{4,5},{5,6},{6,7},{8,9},{9,10},{10,11},{12,13},{... | collective-permute-start | bytes 17432 | tf_op jit(solution)/shard_map/ppermute | solution.py:29
  160.1 3.5 %collective-permute-done.32 = f32[3]{0:T(128)S(1)} collective-permute-done((f32[3]{0:T(128)S(1)}, f32[3]{0:T(128)S(1)}, u32[]{:S(2)}, u32[]{:S(2)}) %collective-permute-start.32) | collective-permute-done | bytes 44 | tf_op jit(solution)/shard_map/ppermute | solution.py:165
  163.9 3.3 %collective-permute-done.33 = f32[3]{0:T(128)S(1)} collective-permute-done((f32[3]{0:T(128)S(1)}, f32[3]{0:T(128)S(1)}, u32[]{:S(2)}, u32[]{:S(2)}) %collective-permute-start.33) | collective-permute-done | bytes 44 | tf_op jit(solution)/shard_map/ppermute | solution.py:165
  167.2 4.4 %collective-permute-done.34 = f32[3]{0:T(128)S(1)} collective-permute-done((f32[3]{0:T(128)S(1)}, f32[3]{0:T(128)S(1)}, u32[]{:S(2)}, u32[]{:S(2)}) %collective-permute-start.34) | collective-permute-done | bytes 44 | tf_op jit(solution)/shard_map/ppermute | solution.py:165
  197.7 4.2 %collective-permute-done.38 = f32[1025]{0:T(1024)S(1)} collective-permute-done((f32[1025]{0:T(1024)S(1)}, f32[1025]{0:T(1024)S(1)}, u32[]{:S(2)}, u32[]{:S(2)}) %collective-permute-start.38) | collective-permute-done | bytes 4132 | tf_op jit(solution)/shard_map/ppermute | solution.py:165
  208.7 4.2 %collective-permute-done.42 = f32[22,3,128]{2,1,0:T(4,128)S(1)} collective-permute-done((f32[22,3,128]{2,1,0:T(4,128)S(1)}, f32[22,3,128]{2,1,0:T(4,128)S(1)}, u32[]{:S(2)}, u32[]{:S(2)}) %collective-permute-start.42) | collective-permute-done | bytes 33824 | tf_op jit(solution)/shard_map/ppermute | solution.py:30
  219.9 4.1 %collective-permute-done.44 = f32[22,22,3]{2,1,0:T(8,128)S(1)} collective-permute-done((f32[22,22,3]{2,1,0:T(8,128)S(1)}, f32[22,22,3]{2,1,0:T(8,128)S(1)}, u32[]{:S(2)}, u32[]{:S(2)}) %collective-permute-start.44) | collective-permute-done | bytes 5840 | tf_op jit(solution)/shard_map/ppermute | solution.py:30
  246.6 4.2 %collective-permute-done.53 = f32[1026]{0:T(1024)S(1)} collective-permute-done((f32[1026]{0:T(1024)S(1)}, f32[1026]{0:T(1024)S(1)}, u32[]{:S(2)}, u32[]{:S(2)}) %collective-permute-start.53) | collective-permute-done | bytes 4136 | tf_op jit(solution)/shard_map/ppermute | solution.py:165
  258.6 4.2 %collective-permute-done.47 = f32[22,3,128]{2,1,0:T(4,128)S(1)} collective-permute-done((f32[22,3,128]{2,1,0:T(4,128)S(1)}, f32[22,3,128]{2,1,0:T(4,128)S(1)}, u32[]{:S(2)}, u32[]{:S(2)}) %collective-permute-start.47) | collective-permute-done | bytes 33824 | tf_op jit(solution)/shard_map/ppermute | solution.py:30
  271.5 3.9 %collective-permute-done.49 = f32[22,22,3]{2,1,0:T(8,128)} collective-permute-done((f32[22,22,3]{2,1,0:T(8,128)S(1)}, f32[22,22,3]{2,1,0:T(8,128)}, u32[]{:S(2)}, u32[]{:S(2)}) %collective-permute-start.49) | collective-permute-done | bytes 5840 | tf_op jit(solution)/shard_map/ppermute | solution.py:30
  288.6 3.5 %collective-permute-done.57 = f32[3]{0:T(128)S(1)} collective-permute-done((f32[3]{0:T(128)S(1)}, f32[3]{0:T(128)S(1)}, u32[]{:S(2)}, u32[]{:S(2)}) %collective-permute-start.57) | collective-permute-done | bytes 44 | tf_op jit(solution)/shard_map/ppermute | solution.py:165
  292.4 3.3 %collective-permute-done.58 = f32[3]{0:T(128)S(1)} collective-permute-done((f32[3]{0:T(128)S(1)}, f32[3]{0:T(128)S(1)}, u32[]{:S(2)}, u32[]{:S(2)}) %collective-permute-start.58) | collective-permute-done | bytes 44 | tf_op jit(solution)/shard_map/ppermute | solution.py:165
  295.6 4.4 %collective-permute-done.59 = f32[3]{0:T(128)S(1)} collective-permute-done((f32[3]{0:T(128)S(1)}, f32[3]{0:T(128)S(1)}, u32[]{:S(2)}, u32[]{:S(2)}) %collective-permute-start.59) | collective-permute-done | bytes 44 | tf_op jit(solution)/shard_map/ppermute | solution.py:165
  (347 shorter events, 187.7 us)
Async XLA Ops:
  1.4 14.6 %collective-permute-start = (f32[2,2,16,128]{3,2,1,0:T(8,128)S(1)}, f32[2,2,16,128]{3,2,1,0:T(8,128)S(1)}, u32[]{:S(2)}, u32[]{:S(2)}) collective-permute-start(f32[2,2,16,128]{3,2,1,0:T(8,128)S(1)} %fusion.78), channel_id=1, source_target_pairs={{0,16},{16,0},{1,17},{17,1},{2,18},{18,2},{3,19},{19,3},{4,20},{20... | collective-permute-start | bytes 98312 | tf_op jit(solution)/shard_map/ppermute | solution.py:22
  3.6 6.2 %collective-permute-start.15 = (f32[1,2,16,130]{3,2,1,0:T(8,128)S(1)}, f32[1,2,16,130]{3,2,1,0:T(8,128)S(1)}, u32[]{:S(2)}, u32[]{:S(2)}) collective-permute-start(f32[1,2,16,130]{3,2,1,0:T(8,128)S(1)} %fusion.77), channel_id=1, source_target_pairs={{0,16},{16,0},{1,17},{17,1},{2,18},{18,2},{3,19},{19,3},{4,20},{20... | collective-permute-start | bytes 49928 | tf_op jit(solution)/shard_map/ppermute | solution.py:22
  9.8 12.1 %collective-permute-start.16 = (f32[4,1,16,130]{3,2,1,0:T(8,128)S(1)}, f32[4,1,16,130]{3,2,1,0:T(8,128)S(1)}, u32[]{:S(2)}, u32[]{:S(2)}) collective-permute-start(f32[4,1,16,130]{3,2,1,0:T(8,128)S(1)} %get-tuple-element.40), channel_id=1, source_target_pairs={{0,4},{4,8},{8,12},{1,5},{5,9},{9,13},{2,6},{6,10},{10,14},{3,7},{... | collective-permute-start | bytes 99848 | tf_op jit(solution)/shard_map/ppermute | solution.py:29
  14.7 7.3 %collective-permute-start.17 = (f32[4,1,16,130]{3,2,1,0:T(8,128)S(1)}, f32[4,1,16,130]{3,2,1,0:T(8,128)S(1)}, u32[]{:S(2)}, u32[]{:S(2)}) collective-permute-start(f32[4,1,16,130]{3,2,1,0:T(8,128)S(1)} %get-tuple-element.41), channel_id=1, source_target_pairs={{4,0},{8,4},{12,8},{5,1},{9,5},{13,9},{6,2},{10,6},{14,10},{7,3},{... | collective-permute-start | bytes 99848 | tf_op jit(solution)/shard_map/ppermute | solution.py:30
  16.1 10.7 %collective-permute-start.1 = (f32[2,20,2,128]{3,2,1,0:T(2,128)S(1)}, f32[2,20,2,128]{3,2,1,0:T(2,128)S(1)}, u32[]{:S(2)}, u32[]{:S(2)}) collective-permute-start(f32[2,20,2,128]{3,2,1,0:T(2,128)S(1)} %get-tuple-element.20), channel_id=1, source_target_pairs={{0,4},{4,8},{8,12},{1,5},{5,9},{9,13},{2,6},{6,10},{10,14},{3,7},{... | collective-permute-start | bytes 122888 | tf_op jit(solution)/shard_map/ppermute | solution.py:29
  20.6 6.3 %collective-permute-start.2 = (f32[2,20,2,128]{3,2,1,0:T(2,128)S(1)}, f32[2,20,2,128]{3,2,1,0:T(2,128)S(1)}, u32[]{:S(2)}, u32[]{:S(2)}) collective-permute-start(f32[2,20,2,128]{3,2,1,0:T(2,128)S(1)} %get-tuple-element.21), channel_id=1, source_target_pairs={{4,0},{8,4},{12,8},{5,1},{9,5},{13,9},{6,2},{10,6},{14,10},{7,3},{... | collective-permute-start | bytes 122888 | tf_op jit(solution)/shard_map/ppermute | solution.py:30
  22.0 11.9 %collective-permute-start.18 = (f32[4,4,1,130]{3,2,1,0:T(1,128)S(1)}, f32[4,4,1,130]{3,2,1,0:T(1,128)S(1)}, u32[]{:S(2)}, u32[]{:S(2)}) collective-permute-start(f32[4,4,1,130]{3,2,1,0:T(1,128)S(1)} %get-tuple-element.30), channel_id=1, source_target_pairs={{0,1},{1,2},{2,3},{4,5},{5,6},{6,7},{8,9},{9,10},{10,11},{12,13},{... | collective-permute-start | bytes 24968 | tf_op jit(solution)/shard_map/ppermute | solution.py:29
  25.5 8.4 %collective-permute-start.19 = (f32[4,4,1,130]{3,2,1,0:T(1,128)S(1)}, f32[4,4,1,130]{3,2,1,0:T(1,128)S(1)}, u32[]{:S(2)}, u32[]{:S(2)}) collective-permute-start(f32[4,4,1,130]{3,2,1,0:T(1,128)S(1)} %get-tuple-element.31), channel_id=1, source_target_pairs={{1,0},{2,1},{3,2},{5,4},{6,5},{7,6},{9,8},{10,9},{11,10},{13,12},{... | collective-permute-start | bytes 24968 | tf_op jit(solution)/shard_map/ppermute | solution.py:30
  28.1 14.0 %collective-permute-start.3 = (f32[2,20,20,2]{3,2,1,0:T(8,128)}, f32[2,20,20,2]{3,2,1,0:T(8,128)S(1)}, u32[]{:S(2)}, u32[]{:S(2)}) collective-permute-start(f32[2,20,20,2]{3,2,1,0:T(8,128)} %get-tuple-element.18), channel_id=1, source_target_pairs={{0,1},{1,2},{2,3},{4,5},{5,6},{6,7},{8,9},{9,10},{10,11},{12,13},{... | collective-permute-start | bytes 19208 | tf_op jit(solution)/shard_map/ppermute | solution.py:29
  32.5 13.6 %collective-permute-start.4 = (f32[2,20,20,2]{3,2,1,0:T(8,128)}, f32[2,20,20,2]{3,2,1,0:T(8,128)S(1)}, u32[]{:S(2)}, u32[]{:S(2)}) collective-permute-start(f32[2,20,20,2]{3,2,1,0:T(8,128)} %get-tuple-element.19), channel_id=1, source_target_pairs={{1,0},{2,1},{3,2},{5,4},{6,5},{7,6},{9,8},{10,9},{11,10},{13,12},{... | collective-permute-start | bytes 19208 | tf_op jit(solution)/shard_map/ppermute | solution.py:30
  53.1 5.0 %collective-permute-start.5 = (f32[1025]{0:T(1024)S(1)}, f32[1025]{0:T(1024)S(1)}, u32[]{:S(2)}, u32[]{:S(2)}) collective-permute-start(f32[1025]{0:T(1024)S(1)} %pad_maximum_fusion.32), channel_id=1, source_target_pairs={{0,4},{4,0},{8,12},{12,8},{1,5},{5,1},{9,13},{13,9},{2,6},{6,2},{1... | collective-permute-start | bytes 12308 | tf_op jit(solution)/shard_map/ppermute | solution.py:165
  75.6 6.6 %collective-permute-start.12 = (f32[22,3,128]{2,1,0:T(4,128)S(1)}, f32[22,3,128]{2,1,0:T(4,128)S(1)}, u32[]{:S(2)}, u32[]{:S(2)}) collective-permute-start(f32[22,3,128]{2,1,0:T(4,128)S(1)} %get-tuple-element.39), channel_id=1, source_target_pairs={{4,0},{8,4},{12,8},{5,1},{9,5},{13,9},{6,2},{10,6},{14,10},{7,3},{... | collective-permute-start | bytes 101384 | tf_op jit(solution)/shard_map/ppermute | solution.py:30
  82.3 8.4 %collective-permute-start.13 = (f32[22,22,3]{2,1,0:T(8,128)S(1)}, f32[22,22,3]{2,1,0:T(8,128)S(1)}, u32[]{:S(2)}, u32[]{:S(2)}) collective-permute-start(f32[22,22,3]{2,1,0:T(8,128)S(1)} %get-tuple-element.28), channel_id=1, source_target_pairs={{0,1},{1,2},{2,3},{4,5},{5,6},{6,7},{8,9},{9,10},{10,11},{12,13},{... | collective-permute-start | bytes 17432 | tf_op jit(solution)/shard_map/ppermute | solution.py:29
  85.8 9.0 %collective-permute-start.14 = (f32[22,22,3]{2,1,0:T(8,128)S(1)}, f32[22,22,3]{2,1,0:T(8,128)S(1)}, u32[]{:S(2)}, u32[]{:S(2)}) collective-permute-start(f32[22,22,3]{2,1,0:T(8,128)S(1)} %get-tuple-element.29), channel_id=1, source_target_pairs={{1,0},{2,1},{3,2},{5,4},{6,5},{7,6},{9,8},{10,9},{11,10},{13,12},{... | collective-permute-start | bytes 17432 | tf_op jit(solution)/shard_map/ppermute | solution.py:30
  123.2 5.6 %collective-permute-start.21 = (f32[22,3,128]{2,1,0:T(4,128)S(1)}, f32[22,3,128]{2,1,0:T(4,128)S(1)}, u32[]{:S(2)}, u32[]{:S(2)}) collective-permute-start(f32[22,3,128]{2,1,0:T(4,128)S(1)} %get-tuple-element.36), channel_id=1, source_target_pairs={{0,4},{4,8},{8,12},{1,5},{5,9},{9,13},{2,6},{6,10},{10,14},{3,7},{... | collective-permute-start | bytes 101384 | tf_op jit(solution)/shard_map/ppermute | solution.py:29
  127.1 5.9 %collective-permute-start.22 = (f32[22,3,128]{2,1,0:T(4,128)S(1)}, f32[22,3,128]{2,1,0:T(4,128)S(1)}, u32[]{:S(2)}, u32[]{:S(2)}) collective-permute-start(f32[22,3,128]{2,1,0:T(4,128)S(1)} %get-tuple-element.37), channel_id=1, source_target_pairs={{4,0},{8,4},{12,8},{5,1},{9,5},{13,9},{6,2},{10,6},{14,10},{7,3},{... | collective-permute-start | bytes 101384 | tf_op jit(solution)/shard_map/ppermute | solution.py:30
  134.6 8.4 %collective-permute-start.23 = (f32[22,22,3]{2,1,0:T(8,128)}, f32[22,22,3]{2,1,0:T(8,128)S(1)}, u32[]{:S(2)}, u32[]{:S(2)}) collective-permute-start(f32[22,22,3]{2,1,0:T(8,128)} %get-tuple-element.26), channel_id=1, source_target_pairs={{0,1},{1,2},{2,3},{4,5},{5,6},{6,7},{8,9},{9,10},{10,11},{12,13},{... | collective-permute-start | bytes 17432 | tf_op jit(solution)/shard_map/ppermute | solution.py:29
  138.0 8.8 %collective-permute-start.24 = (f32[22,22,3]{2,1,0:T(8,128)S(1)}, f32[22,22,3]{2,1,0:T(8,128)}, u32[]{:S(2)}, u32[]{:S(2)}) collective-permute-start(f32[22,22,3]{2,1,0:T(8,128)S(1)} %get-tuple-element.27), channel_id=1, source_target_pairs={{1,0},{2,1},{3,2},{5,4},{6,5},{7,6},{9,8},{10,9},{11,10},{13,12},{... | collective-permute-start | bytes 17432 | tf_op jit(solution)/shard_map/ppermute | solution.py:30
  207.0 5.9 %collective-permute-start.42 = (f32[22,3,128]{2,1,0:T(4,128)S(1)}, f32[22,3,128]{2,1,0:T(4,128)S(1)}, u32[]{:S(2)}, u32[]{:S(2)}) collective-permute-start(f32[22,3,128]{2,1,0:T(4,128)S(1)} %get-tuple-element.35), channel_id=1, source_target_pairs={{4,0},{8,4},{12,8},{5,1},{9,5},{13,9},{6,2},{10,6},{14,10},{7,3},{... | collective-permute-start | bytes 101384 | tf_op jit(solution)/shard_map/ppermute | solution.py:30
  213.1 6.8 %collective-permute-start.43 = (f32[22,22,3]{2,1,0:T(8,128)S(1)}, f32[22,22,3]{2,1,0:T(8,128)S(1)}, u32[]{:S(2)}, u32[]{:S(2)}) collective-permute-start(f32[22,22,3]{2,1,0:T(8,128)S(1)} %get-tuple-element.24), channel_id=1, source_target_pairs={{0,1},{1,2},{2,3},{4,5},{5,6},{6,7},{8,9},{9,10},{10,11},{12,13},{... | collective-permute-start | bytes 17432 | tf_op jit(solution)/shard_map/ppermute | solution.py:29
  215.3 8.7 %collective-permute-start.44 = (f32[22,22,3]{2,1,0:T(8,128)S(1)}, f32[22,22,3]{2,1,0:T(8,128)S(1)}, u32[]{:S(2)}, u32[]{:S(2)}) collective-permute-start(f32[22,22,3]{2,1,0:T(8,128)S(1)} %get-tuple-element.25), channel_id=1, source_target_pairs={{1,0},{2,1},{3,2},{5,4},{6,5},{7,6},{9,8},{10,9},{11,10},{13,12},{... | collective-permute-start | bytes 17432 | tf_op jit(solution)/shard_map/ppermute | solution.py:30
  256.9 5.9 %collective-permute-start.47 = (f32[22,3,128]{2,1,0:T(4,128)S(1)}, f32[22,3,128]{2,1,0:T(4,128)S(1)}, u32[]{:S(2)}, u32[]{:S(2)}) collective-permute-start(f32[22,3,128]{2,1,0:T(4,128)S(1)} %get-tuple-element.33), channel_id=1, source_target_pairs={{4,0},{8,4},{12,8},{5,1},{9,5},{13,9},{6,2},{10,6},{14,10},{7,3},{... | collective-permute-start | bytes 101384 | tf_op jit(solution)/shard_map/ppermute | solution.py:30
  264.4 7.1 %collective-permute-start.48 = (f32[22,22,3]{2,1,0:T(8,128)}, f32[22,22,3]{2,1,0:T(8,128)S(1)}, u32[]{:S(2)}, u32[]{:S(2)}) collective-permute-start(f32[22,22,3]{2,1,0:T(8,128)} %get-tuple-element.22), channel_id=1, source_target_pairs={{0,1},{1,2},{2,3},{4,5},{5,6},{6,7},{8,9},{9,10},{10,11},{12,13},{... | collective-permute-start | bytes 17432 | tf_op jit(solution)/shard_map/ppermute | solution.py:29
  266.6 8.8 %collective-permute-start.49 = (f32[22,22,3]{2,1,0:T(8,128)S(1)}, f32[22,22,3]{2,1,0:T(8,128)}, u32[]{:S(2)}, u32[]{:S(2)}) collective-permute-start(f32[22,22,3]{2,1,0:T(8,128)S(1)} %get-tuple-element.23), channel_id=1, source_target_pairs={{1,0},{2,1},{3,2},{5,4},{6,5},{7,6},{9,8},{10,9},{11,10},{13,12},{... | collective-permute-start | bytes 17432 | tf_op jit(solution)/shard_map/ppermute | solution.py:30
  (54 other events, 447.5 us)
where the time goes:
time: 311 us; the launch traced here: 309 us
  waiting for transfers between devices  113 us (36%)
  starting transfers between devices  82.6 us (27%)
  other arithmetic  32.6 us (10%)
  matrix products  30.4 us (10%)
  local copies, waits for them, and re-layouts  29.3 us (9%)
  between operations  20.9 us (7%)
    ppermute x26, waiting for transfers between devices, butterfly(): lax.ppermute(value, axis, [(i, i ^ step) for i in range(size)])  62.9 us
    ppermute x12, starting transfers between devices, padded_2(): before = lax.ppermute(last, axis, up)  41.6 us
    ppermute x12, waiting for transfers between devices, padded_2(): after = lax.ppermute(leading, axis, down)  37.2 us
    ppermute x26, starting transfers between devices, butterfly(): lax.ppermute(value, axis, [(i, i ^ step) for i in range(size)])  22.2 us
    ppermute x12, starting transfers between devices, padded_2(): after = lax.ppermute(leading, axis, down)  16.2 us
    ppermute x12, waiting for transfers between devices, padded_2(): before = lax.ppermute(last, axis, up)  12.1 us
    reshape x4, local copies, waits for them, and re-layouts, coarse_terms(): field.reshape(count_x, PTS, count_y, PTS, count_z, PTS)  9.93 us
    reduce_sum x4, other arithmetic, coarse_terms(): jnp.mean(field.reshape(count_x, PTS, count_y, PTS, count_z, PTS), axis=(1...  7.3 us
  transfers between devices with their start and end apart: 60, of which 48 were waited for; matrix products, arithmetic and copies ran while one was open for 10% of the time, Pallas kernels for 0%

commit v1 on v0

--- a/solution.py
+++ b/solution.py
@@ -113,8 +113,11 @@
     count_y = field.shape[1] // PTS
     count_z = field.shape[2] // PTS
     cells = count_x * count_y * count_z
-    means = jnp.mean(field.reshape(count_x, PTS, count_y, PTS, count_z, PTS), axis=(1, 3, 5))
-    restricted = means.reshape(cells)
+    point = jnp.arange(field.shape[2], dtype=jnp.int32)
+    along = (point[:, None] // PTS == jnp.arange(count_z, dtype=jnp.int32)[None, :]).astype(jnp.float32)
+    sums = jnp.einsum("pqr,rc->pqc", field, along, precision=PRECISE)
+    sums = jnp.sum(sums.reshape(count_x, PTS, count_y, PTS, count_z), axis=(1, 3))
+    restricted = sums.reshape(cells) * (1.0 / PTS**3)
     terms = jnp.einsum("kpq,p->kq", blocks, restricted, precision=PRECISE)
     return jnp.einsum("kj,kq->jq", selector, terms, precision=PRECISE)
 

time: 311 us -> 307 us (0.987)
  other arithmetic: 32.6 us -> 28.7 us
    reshape x4 -> x0, local copies, waits for them, and re-layouts: 9.93 us -> none  [coarse_terms(): field.reshape(count_x, PTS, count_y, PTS, count_z, PTS)]
    unnamed x36 -> x126, local copies, waits for them, and re-layouts: 3.6 us -> 9.5 us
    reduce_sum x4 -> x6, other arithmetic: 7.3 us -> 3 us  [the longest x4 1.59 us: coarse_terms(): jnp.sum(sums.reshape(count_x, PTS, count_y, PTS, count_z), axis=(1, 3))]
  transfers between devices with their start and end apart: 60 -> 60, of which waited for: 48 -> 46; matrix products, arithmetic and copies ran while one was open for 10% -> 10% of each run, Pallas kernels for 0% -> 0%
where the time goes in v1:
time: 307 us; the launch traced here: 305 us
  waiting for transfers between devices  112 us (36%)
  starting transfers between devices  81.3 us (26%)
  matrix products  33.3 us (11%)
  other arithmetic  28.7 us (9%)
  local copies, waits for them, and re-layouts  27.8 us (9%)
  between operations  21 us (7%)
    ppermute x26, waiting for transfers between devices, butterfly(): lax.ppermute(value, axis, [(i, i ^ step) for i in range(size)])  63.5 us
    ppermute x12, starting transfers between devices, padded_2(): before = lax.ppermute(last, axis, up)  41.2 us
    ppermute x12, waiting for transfers between devices, padded_2(): after = lax.ppermute(leading, axis, down)  37.5 us
    ppermute x26, starting transfers between devices, butterfly(): lax.ppermute(value, axis, [(i, i ^ step) for i in range(size)])  21.3 us
    ppermute x12, starting transfers between devices, padded_2(): after = lax.ppermute(leading, axis, down)  16.2 us
    ppermute x12, waiting for transfers between devices, padded_2(): before = lax.ppermute(last, axis, up)  10.1 us
    unnamed x126, local copies, waits for them, and re-layouts  9.5 us
    dot_general x4, matrix products, spread_rim(): jnp.einsum('pbr,qb->pqr', out, table(shape[1], grid[1]), precision=PRECISE)  6.16 us
  transfers between devices with their start and end apart: 60, of which 46 were waited for; matrix products, arithmetic and copies ran while one was open for 10% of the time, Pallas kernels for 0%

profile of v1, /device:TPU:0, one launch (start us, length us, event | category | flops | bytes accessed | tf_op | source)
XLA Modules:
  0.0 304.6 jit_solution(11254768592436302554)
XLA Ops:
  8.3 4.6 %collective-permute-start.16 = (f32[4,1,16,130]{3,2,1,0:T(8,128)S(1)}, f32[4,1,16,130]{3,2,1,0:T(8,128)S(1)}, u32[]{:S(2)}, u32[]{:S(2)}) collective-permute-start(f32[4,1,16,130]{3,2,1,0:T(8,128)S(1)} %get-tuple-element.34), channel_id=1, source_target_pairs={{0,4},{4,8},{8,12},{1,5},{5,9},{9,13},{2,6},{6,10},{10,14},{3,7},{... | collective-permute-start | bytes 99848 | tf_op jit(solution)/shard_map/ppermute | solution.py:29
  14.3 4.5 %collective-permute-start.1 = (f32[2,20,2,128]{3,2,1,0:T(2,128)S(1)}, f32[2,20,2,128]{3,2,1,0:T(2,128)S(1)}, u32[]{:S(2)}, u32[]{:S(2)}) collective-permute-start(f32[2,20,2,128]{3,2,1,0:T(2,128)S(1)} %get-tuple-element.14), channel_id=1, source_target_pairs={{0,4},{4,8},{8,12},{1,5},{5,9},{9,13},{2,6},{6,10},{10,14},{3,7},{... | collective-permute-start | bytes 122888 | tf_op jit(solution)/shard_map/ppermute | solution.py:29
  20.2 3.5 %collective-permute-start.18 = (f32[4,4,1,130]{3,2,1,0:T(1,128)S(1)}, f32[4,4,1,130]{3,2,1,0:T(1,128)S(1)}, u32[]{:S(2)}, u32[]{:S(2)}) collective-permute-start(f32[4,4,1,130]{3,2,1,0:T(1,128)S(1)} %get-tuple-element.24), channel_id=1, source_target_pairs={{0,1},{1,2},{2,3},{4,5},{5,6},{6,7},{8,9},{9,10},{10,11},{12,13},{... | collective-permute-start | bytes 24968 | tf_op jit(solution)/shard_map/ppermute | solution.py:29
  26.3 4.5 %collective-permute-start.3 = (f32[2,20,20,2]{3,2,1,0:T(8,128)}, f32[2,20,20,2]{3,2,1,0:T(8,128)S(1)}, u32[]{:S(2)}, u32[]{:S(2)}) collective-permute-start(f32[2,20,20,2]{3,2,1,0:T(8,128)} %get-tuple-element.12), channel_id=1, source_target_pairs={{0,1},{1,2},{2,3},{4,5},{5,6},{6,7},{8,9},{9,10},{10,11},{12,13},{... | collective-permute-start | bytes 19208 | tf_op jit(solution)/shard_map/ppermute | solution.py:29
  34.0 6.7 %collective-permute-done.3 = f32[2,20,20,2]{3,2,1,0:T(8,128)S(1)} collective-permute-done((f32[2,20,20,2]{3,2,1,0:T(8,128)}, f32[2,20,20,2]{3,2,1,0:T(8,128)S(1)}, u32[]{:S(2)}, u32[]{:S(2)}) %collective-permute-start.3) | collective-permute-done | bytes 6432 | tf_op jit(solution)/shard_map/ppermute | solution.py:29
  40.8 4.0 %collective-permute-done.4 = f32[2,20,20,2]{3,2,1,0:T(8,128)S(1)} collective-permute-done((f32[2,20,20,2]{3,2,1,0:T(8,128)}, f32[2,20,20,2]{3,2,1,0:T(8,128)S(1)}, u32[]{:S(2)}, u32[]{:S(2)}) %collective-permute-start.4) | collective-permute-done | bytes 6432 | tf_op jit(solution)/shard_map/ppermute | solution.py:30
  72.6 4.9 %collective-permute-done.12 = f32[22,3,128]{2,1,0:T(4,128)S(1)} collective-permute-done((f32[22,3,128]{2,1,0:T(4,128)S(1)}, f32[22,3,128]{2,1,0:T(4,128)S(1)}, u32[]{:S(2)}, u32[]{:S(2)}) %collective-permute-start.12) | collective-permute-done | bytes 33824 | tf_op jit(solution)/shard_map/ppermute | solution.py:30
  77.6 3.5 %collective-permute-start.13 = (f32[22,22,3]{2,1,0:T(8,128)S(1)}, f32[22,22,3]{2,1,0:T(8,128)S(1)}, u32[]{:S(2)}, u32[]{:S(2)}) collective-permute-start(f32[22,22,3]{2,1,0:T(8,128)S(1)} %get-tuple-element.22), channel_id=1, source_target_pairs={{0,1},{1,2},{2,3},{4,5},{5,6},{6,7},{8,9},{9,10},{10,11},{12,13},{... | collective-permute-start | bytes 17432 | tf_op jit(solution)/shard_map/ppermute | solution.py:29
  86.0 4.1 %collective-permute-done.14 = f32[22,22,3]{2,1,0:T(8,128)S(1)} collective-permute-done((f32[22,22,3]{2,1,0:T(8,128)S(1)}, f32[22,22,3]{2,1,0:T(8,128)S(1)}, u32[]{:S(2)}, u32[]{:S(2)}) %collective-permute-start.14) | collective-permute-done | bytes 5840 | tf_op jit(solution)/shard_map/ppermute | solution.py:30
  122.0 4.2 %collective-permute-done.22 = f32[22,3,128]{2,1,0:T(4,128)S(1)} collective-permute-done((f32[22,3,128]{2,1,0:T(4,128)S(1)}, f32[22,3,128]{2,1,0:T(4,128)S(1)}, u32[]{:S(2)}, u32[]{:S(2)}) %collective-permute-start.22) | collective-permute-done | bytes 33824 | tf_op jit(solution)/shard_map/ppermute | solution.py:30
  127.8 3.5 %collective-permute-start.23 = (f32[22,22,3]{2,1,0:T(8,128)}, f32[22,22,3]{2,1,0:T(8,128)S(1)}, u32[]{:S(2)}, u32[]{:S(2)}) collective-permute-start(f32[22,22,3]{2,1,0:T(8,128)} %get-tuple-element.20), channel_id=1, source_target_pairs={{0,1},{1,2},{2,3},{4,5},{5,6},{6,7},{8,9},{9,10},{10,11},{12,13},{... | collective-permute-start | bytes 17432 | tf_op jit(solution)/shard_map/ppermute | solution.py:29
  136.9 3.2 %collective-permute-done.24 = f32[22,22,3]{2,1,0:T(8,128)} collective-permute-done((f32[22,22,3]{2,1,0:T(8,128)S(1)}, f32[22,22,3]{2,1,0:T(8,128)}, u32[]{:S(2)}, u32[]{:S(2)}) %collective-permute-start.24) | collective-permute-done | bytes 5840 | tf_op jit(solution)/shard_map/ppermute | solution.py:30
  153.3 3.5 %collective-permute-done.32 = f32[3]{0:T(128)S(1)} collective-permute-done((f32[3]{0:T(128)S(1)}, f32[3]{0:T(128)S(1)}, u32[]{:S(2)}, u32[]{:S(2)}) %collective-permute-start.32) | collective-permute-done | bytes 44 | tf_op jit(solution)/shard_map/ppermute | solution.py:168
  157.1 3.3 %collective-permute-done.33 = f32[3]{0:T(128)S(1)} collective-permute-done((f32[3]{0:T(128)S(1)}, f32[3]{0:T(128)S(1)}, u32[]{:S(2)}, u32[]{:S(2)}) %collective-permute-start.33) | collective-permute-done | bytes 44 | tf_op jit(solution)/shard_map/ppermute | solution.py:168
  160.4 4.4 %collective-permute-done.34 = f32[3]{0:T(128)S(1)} collective-permute-done((f32[3]{0:T(128)S(1)}, f32[3]{0:T(128)S(1)}, u32[]{:S(2)}, u32[]{:S(2)}) %collective-permute-start.34) | collective-permute-done | bytes 44 | tf_op jit(solution)/shard_map/ppermute | solution.py:168
  188.9 4.2 %collective-permute-done.38 = f32[1025]{0:T(1024)S(1)} collective-permute-done((f32[1025]{0:T(1024)S(1)}, f32[1025]{0:T(1024)S(1)}, u32[]{:S(2)}, u32[]{:S(2)}) %collective-permute-start.38) | collective-permute-done | bytes 4132 | tf_op jit(solution)/shard_map/ppermute | solution.py:168
  200.5 4.2 %collective-permute-done.42 = f32[22,3,128]{2,1,0:T(4,128)S(1)} collective-permute-done((f32[22,3,128]{2,1,0:T(4,128)S(1)}, f32[22,3,128]{2,1,0:T(4,128)S(1)}, u32[]{:S(2)}, u32[]{:S(2)}) %collective-permute-start.42) | collective-permute-done | bytes 33824 | tf_op jit(solution)/shard_map/ppermute | solution.py:30
  211.7 4.1 %collective-permute-done.44 = f32[22,22,3]{2,1,0:T(8,128)S(1)} collective-permute-done((f32[22,22,3]{2,1,0:T(8,128)S(1)}, f32[22,22,3]{2,1,0:T(8,128)S(1)}, u32[]{:S(2)}, u32[]{:S(2)}) %collective-permute-start.44) | collective-permute-done | bytes 5840 | tf_op jit(solution)/shard_map/ppermute | solution.py:30
  241.9 4.2 %collective-permute-done.53 = f32[1026]{0:T(1024)S(1)} collective-permute-done((f32[1026]{0:T(1024)S(1)}, f32[1026]{0:T(1024)S(1)}, u32[]{:S(2)}, u32[]{:S(2)}) %collective-permute-start.53) | collective-permute-done | bytes 4136 | tf_op jit(solution)/shard_map/ppermute | solution.py:168
  254.4 4.2 %collective-permute-done.47 = f32[22,3,128]{2,1,0:T(4,128)S(1)} collective-permute-done((f32[22,3,128]{2,1,0:T(4,128)S(1)}, f32[22,3,128]{2,1,0:T(4,128)S(1)}, u32[]{:S(2)}, u32[]{:S(2)}) %collective-permute-start.47) | collective-permute-done | bytes 33824 | tf_op jit(solution)/shard_map/ppermute | solution.py:30
  266.3 4.3 %collective-permute-done.49 = f32[22,22,3]{2,1,0:T(8,128)} collective-permute-done((f32[22,22,3]{2,1,0:T(8,128)S(1)}, f32[22,22,3]{2,1,0:T(8,128)}, u32[]{:S(2)}, u32[]{:S(2)}) %collective-permute-start.49) | collective-permute-done | bytes 5840 | tf_op jit(solution)/shard_map/ppermute | solution.py:30
  283.9 3.5 %collective-permute-done.57 = f32[3]{0:T(128)S(1)} collective-permute-done((f32[3]{0:T(128)S(1)}, f32[3]{0:T(128)S(1)}, u32[]{:S(2)}, u32[]{:S(2)}) %collective-permute-start.57) | collective-permute-done | bytes 44 | tf_op jit(solution)/shard_map/ppermute | solution.py:168
  287.5 3.5 %collective-permute-done.58 = f32[3]{0:T(128)S(1)} collective-permute-done((f32[3]{0:T(128)S(1)}, f32[3]{0:T(128)S(1)}, u32[]{:S(2)}, u32[]{:S(2)}) %collective-permute-start.58) | collective-permute-done | bytes 44 | tf_op jit(solution)/shard_map/ppermute | solution.py:168
  291.0 4.4 %collective-permute-done.59 = f32[3]{0:T(128)S(1)} collective-permute-done((f32[3]{0:T(128)S(1)}, f32[3]{0:T(128)S(1)}, u32[]{:S(2)}, u32[]{:S(2)}) %collective-permute-start.59) | collective-permute-done | bytes 44 | tf_op jit(solution)/shard_map/ppermute | solution.py:168
  (439 shorter events, 184.2 us)
Async XLA Ops:
  1.5 12.7 %collective-permute-start = (f32[2,2,16,128]{3,2,1,0:T(8,128)S(1)}, f32[2,2,16,128]{3,2,1,0:T(8,128)S(1)}, u32[]{:S(2)}, u32[]{:S(2)}) collective-permute-start(f32[2,2,16,128]{3,2,1,0:T(8,128)S(1)} %fusion.86), channel_id=1, source_target_pairs={{0,16},{16,0},{1,17},{17,1},{2,18},{18,2},{3,19},{19,3},{4,20},{20... | collective-permute-start | bytes 98312 | tf_op jit(solution)/shard_map/ppermute | solution.py:22
  2.7 5.6 %collective-permute-start.15 = (f32[1,2,16,130]{3,2,1,0:T(8,128)S(1)}, f32[1,2,16,130]{3,2,1,0:T(8,128)S(1)}, u32[]{:S(2)}, u32[]{:S(2)}) collective-permute-start(f32[1,2,16,130]{3,2,1,0:T(8,128)S(1)} %fusion.85), channel_id=1, source_target_pairs={{0,16},{16,0},{1,17},{17,1},{2,18},{18,2},{3,19},{19,3},{4,20},{20... | collective-permute-start | bytes 49928 | tf_op jit(solution)/shard_map/ppermute | solution.py:22
  8.3 11.8 %collective-permute-start.16 = (f32[4,1,16,130]{3,2,1,0:T(8,128)S(1)}, f32[4,1,16,130]{3,2,1,0:T(8,128)S(1)}, u32[]{:S(2)}, u32[]{:S(2)}) collective-permute-start(f32[4,1,16,130]{3,2,1,0:T(8,128)S(1)} %get-tuple-element.34), channel_id=1, source_target_pairs={{0,4},{4,8},{8,12},{1,5},{5,9},{9,13},{2,6},{6,10},{10,14},{3,7},{... | collective-permute-start | bytes 99848 | tf_op jit(solution)/shard_map/ppermute | solution.py:29
  12.9 7.3 %collective-permute-start.17 = (f32[4,1,16,130]{3,2,1,0:T(8,128)S(1)}, f32[4,1,16,130]{3,2,1,0:T(8,128)S(1)}, u32[]{:S(2)}, u32[]{:S(2)}) collective-permute-start(f32[4,1,16,130]{3,2,1,0:T(8,128)S(1)} %get-tuple-element.35), channel_id=1, source_target_pairs={{4,0},{8,4},{12,8},{5,1},{9,5},{13,9},{6,2},{10,6},{14,10},{7,3},{... | collective-permute-start | bytes 99848 | tf_op jit(solution)/shard_map/ppermute | solution.py:30
  14.3 10.7 %collective-permute-start.1 = (f32[2,20,2,128]{3,2,1,0:T(2,128)S(1)}, f32[2,20,2,128]{3,2,1,0:T(2,128)S(1)}, u32[]{:S(2)}, u32[]{:S(2)}) collective-permute-start(f32[2,20,2,128]{3,2,1,0:T(2,128)S(1)} %get-tuple-element.14), channel_id=1, source_target_pairs={{0,4},{4,8},{8,12},{1,5},{5,9},{9,13},{2,6},{6,10},{10,14},{3,7},{... | collective-permute-start | bytes 122888 | tf_op jit(solution)/shard_map/ppermute | solution.py:29
  18.8 6.3 %collective-permute-start.2 = (f32[2,20,2,128]{3,2,1,0:T(2,128)S(1)}, f32[2,20,2,128]{3,2,1,0:T(2,128)S(1)}, u32[]{:S(2)}, u32[]{:S(2)}) collective-permute-start(f32[2,20,2,128]{3,2,1,0:T(2,128)S(1)} %get-tuple-element.15), channel_id=1, source_target_pairs={{4,0},{8,4},{12,8},{5,1},{9,5},{13,9},{6,2},{10,6},{14,10},{7,3},{... | collective-permute-start | bytes 122888 | tf_op jit(solution)/shard_map/ppermute | solution.py:30
  20.2 11.9 %collective-permute-start.18 = (f32[4,4,1,130]{3,2,1,0:T(1,128)S(1)}, f32[4,4,1,130]{3,2,1,0:T(1,128)S(1)}, u32[]{:S(2)}, u32[]{:S(2)}) collective-permute-start(f32[4,4,1,130]{3,2,1,0:T(1,128)S(1)} %get-tuple-element.24), channel_id=1, source_target_pairs={{0,1},{1,2},{2,3},{4,5},{5,6},{6,7},{8,9},{9,10},{10,11},{12,13},{... | collective-permute-start | bytes 24968 | tf_op jit(solution)/shard_map/ppermute | solution.py:29
  23.7 8.4 %collective-permute-start.19 = (f32[4,4,1,130]{3,2,1,0:T(1,128)S(1)}, f32[4,4,1,130]{3,2,1,0:T(1,128)S(1)}, u32[]{:S(2)}, u32[]{:S(2)}) collective-permute-start(f32[4,4,1,130]{3,2,1,0:T(1,128)S(1)} %get-tuple-element.25), channel_id=1, source_target_pairs={{1,0},{2,1},{3,2},{5,4},{6,5},{7,6},{9,8},{10,9},{11,10},{13,12},{... | collective-permute-start | bytes 24968 | tf_op jit(solution)/shard_map/ppermute | solution.py:30
  26.3 14.5 %collective-permute-start.3 = (f32[2,20,20,2]{3,2,1,0:T(8,128)}, f32[2,20,20,2]{3,2,1,0:T(8,128)S(1)}, u32[]{:S(2)}, u32[]{:S(2)}) collective-permute-start(f32[2,20,20,2]{3,2,1,0:T(8,128)} %get-tuple-element.12), channel_id=1, source_target_pairs={{0,1},{1,2},{2,3},{4,5},{5,6},{6,7},{8,9},{9,10},{10,11},{12,13},{... | collective-permute-start | bytes 19208 | tf_op jit(solution)/shard_map/ppermute | solution.py:29
  30.8 14.0 %collective-permute-start.4 = (f32[2,20,20,2]{3,2,1,0:T(8,128)}, f32[2,20,20,2]{3,2,1,0:T(8,128)S(1)}, u32[]{:S(2)}, u32[]{:S(2)}) collective-permute-start(f32[2,20,20,2]{3,2,1,0:T(8,128)} %get-tuple-element.13), channel_id=1, source_target_pairs={{1,0},{2,1},{3,2},{5,4},{6,5},{7,6},{9,8},{10,9},{11,10},{13,12},{... | collective-permute-start | bytes 19208 | tf_op jit(solution)/shard_map/ppermute | solution.py:30
  48.4 5.2 %collective-permute-start.5 = (f32[1025]{0:T(1024)S(1)}, f32[1025]{0:T(1024)S(1)}, u32[]{:S(2)}, u32[]{:S(2)}) collective-permute-start(f32[1025]{0:T(1024)S(1)} %pad_maximum_fusion.32), channel_id=1, source_target_pairs={{0,4},{4,0},{8,12},{12,8},{1,5},{5,1},{9,13},{13,9},{2,6},{6,2},{1... | collective-permute-start | bytes 12308 | tf_op jit(solution)/shard_map/ppermute | solution.py:168
  70.9 6.6 %collective-permute-start.12 = (f32[22,3,128]{2,1,0:T(4,128)S(1)}, f32[22,3,128]{2,1,0:T(4,128)S(1)}, u32[]{:S(2)}, u32[]{:S(2)}) collective-permute-start(f32[22,3,128]{2,1,0:T(4,128)S(1)} %get-tuple-element.33), channel_id=1, source_target_pairs={{4,0},{8,4},{12,8},{5,1},{9,5},{13,9},{6,2},{10,6},{14,10},{7,3},{... | collective-permute-start | bytes 101384 | tf_op jit(solution)/shard_map/ppermute | solution.py:30
  77.6 8.4 %collective-permute-start.13 = (f32[22,22,3]{2,1,0:T(8,128)S(1)}, f32[22,22,3]{2,1,0:T(8,128)S(1)}, u32[]{:S(2)}, u32[]{:S(2)}) collective-permute-start(f32[22,22,3]{2,1,0:T(8,128)S(1)} %get-tuple-element.22), channel_id=1, source_target_pairs={{0,1},{1,2},{2,3},{4,5},{5,6},{6,7},{8,9},{9,10},{10,11},{12,13},{... | collective-permute-start | bytes 17432 | tf_op jit(solution)/shard_map/ppermute | solution.py:29
  81.1 9.0 %collective-permute-start.14 = (f32[22,22,3]{2,1,0:T(8,128)S(1)}, f32[22,22,3]{2,1,0:T(8,128)S(1)}, u32[]{:S(2)}, u32[]{:S(2)}) collective-permute-start(f32[22,22,3]{2,1,0:T(8,128)S(1)} %get-tuple-element.23), channel_id=1, source_target_pairs={{1,0},{2,1},{3,2},{5,4},{6,5},{7,6},{9,8},{10,9},{11,10},{13,12},{... | collective-permute-start | bytes 17432 | tf_op jit(solution)/shard_map/ppermute | solution.py:30
  96.7 5.0 %collective-permute-start.25 = (f32[1026]{0:T(1024)S(1)}, f32[1026]{0:T(1024)S(1)}, u32[]{:S(2)}, u32[]{:S(2)}) collective-permute-start(f32[1026]{0:T(1024)S(1)} %concatenate.83), channel_id=1, source_target_pairs={{0,4},{4,0},{8,12},{12,8},{1,5},{5,1},{9,13},{13,9},{2,6},{6,2},{1... | collective-permute-start | bytes 12320 | tf_op jit(solution)/shard_map/ppermute | solution.py:168
  120.3 5.9 %collective-permute-start.22 = (f32[22,3,128]{2,1,0:T(4,128)S(1)}, f32[22,3,128]{2,1,0:T(4,128)S(1)}, u32[]{:S(2)}, u32[]{:S(2)}) collective-permute-start(f32[22,3,128]{2,1,0:T(4,128)S(1)} %get-tuple-element.31), channel_id=1, source_target_pairs={{4,0},{8,4},{12,8},{5,1},{9,5},{13,9},{6,2},{10,6},{14,10},{7,3},{... | collective-permute-start | bytes 101384 | tf_op jit(solution)/shard_map/ppermute | solution.py:30
  127.8 8.4 %collective-permute-start.23 = (f32[22,22,3]{2,1,0:T(8,128)}, f32[22,22,3]{2,1,0:T(8,128)S(1)}, u32[]{:S(2)}, u32[]{:S(2)}) collective-permute-start(f32[22,22,3]{2,1,0:T(8,128)} %get-tuple-element.20), channel_id=1, source_target_pairs={{0,1},{1,2},{2,3},{4,5},{5,6},{6,7},{8,9},{9,10},{10,11},{12,13},{... | collective-permute-start | bytes 17432 | tf_op jit(solution)/shard_map/ppermute | solution.py:29
  131.3 8.8 %collective-permute-start.24 = (f32[22,22,3]{2,1,0:T(8,128)S(1)}, f32[22,22,3]{2,1,0:T(8,128)}, u32[]{:S(2)}, u32[]{:S(2)}) collective-permute-start(f32[22,22,3]{2,1,0:T(8,128)S(1)} %get-tuple-element.21), channel_id=1, source_target_pairs={{1,0},{2,1},{3,2},{5,4},{6,5},{7,6},{9,8},{10,9},{11,10},{13,12},{... | collective-permute-start | bytes 17432 | tf_op jit(solution)/shard_map/ppermute | solution.py:30
  198.8 5.9 %collective-permute-start.42 = (f32[22,3,128]{2,1,0:T(4,128)S(1)}, f32[22,3,128]{2,1,0:T(4,128)S(1)}, u32[]{:S(2)}, u32[]{:S(2)}) collective-permute-start(f32[22,3,128]{2,1,0:T(4,128)S(1)} %get-tuple-element.29), channel_id=1, source_target_pairs={{4,0},{8,4},{12,8},{5,1},{9,5},{13,9},{6,2},{10,6},{14,10},{7,3},{... | collective-permute-start | bytes 101384 | tf_op jit(solution)/shard_map/ppermute | solution.py:30
  204.9 6.8 %collective-permute-start.43 = (f32[22,22,3]{2,1,0:T(8,128)S(1)}, f32[22,22,3]{2,1,0:T(8,128)S(1)}, u32[]{:S(2)}, u32[]{:S(2)}) collective-permute-start(f32[22,22,3]{2,1,0:T(8,128)S(1)} %get-tuple-element.18), channel_id=1, source_target_pairs={{0,1},{1,2},{2,3},{4,5},{5,6},{6,7},{8,9},{9,10},{10,11},{12,13},{... | collective-permute-start | bytes 17432 | tf_op jit(solution)/shard_map/ppermute | solution.py:29
  207.1 8.7 %collective-permute-start.44 = (f32[22,22,3]{2,1,0:T(8,128)S(1)}, f32[22,22,3]{2,1,0:T(8,128)S(1)}, u32[]{:S(2)}, u32[]{:S(2)}) collective-permute-start(f32[22,22,3]{2,1,0:T(8,128)S(1)} %get-tuple-element.19), channel_id=1, source_target_pairs={{1,0},{2,1},{3,2},{5,4},{6,5},{7,6},{9,8},{10,9},{11,10},{13,12},{... | collective-permute-start | bytes 17432 | tf_op jit(solution)/shard_map/ppermute | solution.py:30
  252.7 5.9 %collective-permute-start.47 = (f32[22,3,128]{2,1,0:T(4,128)S(1)}, f32[22,3,128]{2,1,0:T(4,128)S(1)}, u32[]{:S(2)}, u32[]{:S(2)}) collective-permute-start(f32[22,3,128]{2,1,0:T(4,128)S(1)} %get-tuple-element.27), channel_id=1, source_target_pairs={{4,0},{8,4},{12,8},{5,1},{9,5},{13,9},{6,2},{10,6},{14,10},{7,3},{... | collective-permute-start | bytes 101384 | tf_op jit(solution)/shard_map/ppermute | solution.py:30
  258.9 7.5 %collective-permute-start.48 = (f32[22,22,3]{2,1,0:T(8,128)S(1)}, f32[22,22,3]{2,1,0:T(8,128)}, u32[]{:S(2)}, u32[]{:S(2)}) collective-permute-start(f32[22,22,3]{2,1,0:T(8,128)S(1)} %get-tuple-element.16), channel_id=1, source_target_pairs={{0,1},{1,2},{2,3},{4,5},{5,6},{6,7},{8,9},{9,10},{10,11},{12,13},{... | collective-permute-start | bytes 17432 | tf_op jit(solution)/shard_map/ppermute | solution.py:29
  261.8 8.8 %collective-permute-start.49 = (f32[22,22,3]{2,1,0:T(8,128)S(1)}, f32[22,22,3]{2,1,0:T(8,128)}, u32[]{:S(2)}, u32[]{:S(2)}) collective-permute-start(f32[22,22,3]{2,1,0:T(8,128)S(1)} %get-tuple-element.17), channel_id=1, source_target_pairs={{1,0},{2,1},{3,2},{5,4},{6,5},{7,6},{9,8},{10,9},{11,10},{13,12},{... | collective-permute-start | bytes 17432 | tf_op jit(solution)/shard_map/ppermute | solution.py:30
  (100 other events, 819.2 us)

commit v2 on v1

--- a/solution.py
+++ b/solution.py
@@ -1,3 +1,5 @@
+import functools
+
 import jax
 import jax.numpy as jnp
 from jax import lax
@@ -12,23 +14,27 @@
 PRECISE = lax.Precision.HIGHEST
 
 
+def pad_side(value, axis, dim, width):
+    size, length = (lax.axis_size(axis), value.shape[dim])
+    last = lax.slice_in_dim(value, length - width, length, axis=dim)
+    leading = lax.slice_in_dim(value, 0, width, axis=dim)
+    if size == 2:
+        first = lax.axis_index(axis) == 0
+        got = lax.ppermute(jnp.where(first, last, leading), axis, [(0, 1), (1, 0)])
+        zero = jnp.zeros_like(got)
+        before = jnp.where(first, zero, got)
+        after = jnp.where(first, got, zero)
+    else:
+        up = [(i, (i + 1) % size) for i in range(size - 1)]
+        down = [(j, i) for i, j in up]
+        before = lax.ppermute(last, axis, up)
+        after = lax.ppermute(leading, axis, down)
+    return jnp.concatenate([before, value, after], axis=dim)
+
+
 def padded_2(value, sides, width):
     for axis, dim in sides:
-        size, length = (lax.axis_size(axis), value.shape[dim])
-        last = lax.slice_in_dim(value, length - width, length, axis=dim)
-        leading = lax.slice_in_dim(value, 0, width, axis=dim)
-        if size == 2:
-            first = lax.axis_index(axis) == 0
-            got = lax.ppermute(jnp.where(first, last, leading), axis, [(0, 1), (1, 0)])
-            zero = jnp.zeros_like(got)
-            before = jnp.where(first, zero, got)
-            after = jnp.where(first, got, zero)
-        else:
-            up = [(i, (i + 1) % size) for i in range(size - 1)]
-            down = [(j, i) for i, j in up]
-            before = lax.ppermute(last, axis, up)
-            after = lax.ppermute(leading, axis, down)
-        value = jnp.concatenate([before, value, after], axis=dim)
+        value = pad_side(value, axis, dim, width)
     return value
 
 
@@ -157,16 +163,24 @@
 ALL = ("gx", "ga", "gz")
 
 
-def butterfly(value, axes):
+def butterfly_stages(axes):
+    stages = []
     for axis in axes:
         size = lax.axis_size(axis)
         if size & (size - 1):
-            value = lax.psum(value, axis)
+            stages.append(lambda value, axis=axis: lax.psum(value, axis))
             continue
         step = 1
         while step < size:
-            value = value + lax.ppermute(value, axis, [(i, i ^ step) for i in range(size)])
+            pairs = [(i, i ^ step) for i in range(size)]
+            stages.append(lambda value, axis=axis, pairs=pairs: value + lax.ppermute(value, axis, pairs))
             step *= 2
+    return stages
+
+
+def butterfly(value, axes):
+    for stage in butterfly_stages(axes):
+        value = stage(value)
     return value
 
 
@@ -175,10 +189,21 @@
     return [total[i] for i in range(len(scalars))]
 
 
-def reduce_coarse(buffer, scalars):
+HALO_ORDER = (("ga", 1), ("gz", 2), ("gx", 0))
+
+
+def reduce_coarse(local, buffer, scalars):
     count = len(scalars)
-    payload = lax.optimization_barrier(jnp.concatenate([buffer.reshape(-1), jnp.stack(scalars)]))
-    payload = butterfly(payload, ("ga", "gz"))
+    payload = jnp.concatenate([buffer.reshape(-1), jnp.stack(scalars)])
+    halo = [functools.partial(pad_side, axis=axis, dim=dim, width=RIM + 1) for axis, dim in HALO_ORDER]
+    sums = butterfly_stages(("ga", "gz"))
+    local, payload = lax.optimization_barrier((local, payload))
+    for index in range(max(len(halo), len(sums))):
+        if index < len(halo):
+            local = halo[index](local)
+        if index < len(sums):
+            payload = sums[index](payload)
+        local, payload = lax.optimization_barrier((local, payload))
     size = payload.shape[0] - count
     whole = payload[:size].reshape(buffer.shape)
     if lax.axis_size("gx") == 2:
@@ -194,7 +219,7 @@
         up = [(i, i + 1) for i in range(gx - 1)]
         lo = lax.ppermute(whole, "gx", up)
         hi = lax.ppermute(whole, "gx", [(j, i) for i, j in up])
-    return (lo, whole, hi), [total[i] for i in range(count)]
+    return local, (lo, whole, hi), [total[i] for i in range(count)]
 
 
 def body(right_side, diagonal, basis_tables, eigenvalues, coarse_blocks, coarse_columns):
@@ -212,7 +237,7 @@
 
     def precondition_rim(wide_field, field):
         local = schwarz_part(wide_field, basis_tables, eigenvalues)
-        return padded_2(local, SIDES, RIM + 1), coarse_terms(field, blocks, selector)
+        return local, coarse_terms(field, blocks, selector)
 
     def coarse_on_rim(wholes):
         return spread_rim(coarse_rim(wholes, table, count, group), RIM + 1, shape)
@@ -221,7 +246,7 @@
     for restart in range(CYCLES):
         residual = interior(wide_residual, RIM)
         wide_local, terms = precondition_rim(wide_residual, residual)
-        wholes, (square,) = reduce_coarse(terms, [jnp.sum(residual * residual)])
+        wide_local, wholes, (square,) = reduce_coarse(wide_local, terms, [jnp.sum(residual * residual)])
         initial_norm = jnp.sqrt(square)
         first_vector = residual / initial_norm
         wide_zed = (wide_local + coarse_on_rim(wholes)) / initial_norm
@@ -229,8 +254,8 @@
         wide_first = operate_rim(wide_zed, wide_diagonal, inside)
         first_image = interior(wide_first, RIM)
         wide_local, terms = precondition_rim(wide_first, first_image)
-        wholes, (first_proj, image_square) = reduce_coarse(
-            terms, [jnp.sum(first_vector * first_image), jnp.sum(first_image * first_image)]
+        wide_local, wholes, (first_proj, image_square) = reduce_coarse(
+            wide_local, terms, [jnp.sum(first_vector * first_image), jnp.sum(first_image * first_image)]
         )
         first_len = jnp.sqrt(image_square - first_proj * first_proj)
         second_vector = (first_image - first_proj * first_vector) / first_len

time: 307 us -> 282 us (0.919)
  waiting for transfers between devices: 112 us -> 63.8 us
  starting transfers between devices: 81.3 us -> 121 us
  local copies, waits for them, and re-layouts: 27.8 us -> 17.9 us
  matrix products: 33.3 us -> 23.6 us
  other arithmetic: 28.7 us -> 32.9 us
    ppermute x56, waiting for transfers between devices: 111 us -> 61 us  [the longest x26 41.3 us: butterfly_stages(): lax.ppermute(value, axis, pairs)]
    ppermute x56, starting transfers between devices: 81.3 us -> 121 us  [the longest x12 56.9 us: pad_side(): before = lax.ppermute(last, axis, up)]
    div x0 -> x4, other arithmetic: none -> 4.11 us  [the longest x2 3.97 us: body(): (wide_local + coarse_on_rim(wholes) - first_proj * wide_zed) / first_len]
    unnamed x126 -> x50, local copies, waits for them, and re-layouts: 9.5 us -> 6.16 us
    concatenate x10 -> x18, other arithmetic: 2.26 us -> 5.54 us  [the longest x16 4.39 us: pad_side(): return jnp.concatenate([before, value, after], axis=dim)]
  transfers between devices with their start and end apart: 60 -> 60, of which waited for: 46 -> 33; matrix products, arithmetic and copies ran while one was open for 10% -> 2% of each run, Pallas kernels for 0% -> 0%
where the time goes in v2:
time: 282 us; the launch traced here: 281 us
  starting transfers between devices  121 us (43%)
  waiting for transfers between devices  63.8 us (23%)
  other arithmetic  32.9 us (12%)
  matrix products  23.6 us (8%)
  between operations  21.2 us (8%)
  local copies, waits for them, and re-layouts  17.9 us (6%)
    ppermute x12, starting transfers between devices, pad_side(): before = lax.ppermute(last, axis, up)  56.9 us
    ppermute x26, starting transfers between devices, butterfly_stages(): lax.ppermute(value, axis, pairs)  48 us
    ppermute x26, waiting for transfers between devices, butterfly_stages(): lax.ppermute(value, axis, pairs)  41.3 us
    ppermute x12, starting transfers between devices, pad_side(): after = lax.ppermute(leading, axis, down)  15.5 us
    ppermute x12, waiting for transfers between devices, pad_side(): after = lax.ppermute(leading, axis, down)  10 us
    ppermute x12, waiting for transfers between devices, pad_side(): before = lax.ppermute(last, axis, up)  9.67 us
    unnamed x50, local copies, waits for them, and re-layouts  6.16 us
  transfers between devices with their start and end apart: 60, of which 33 were waited for; matrix products, arithmetic and copies ran while one was open for 2% of the time, Pallas kernels for 0%

profile of v2, /device:TPU:0, one launch (start us, length us, event | category | flops | bytes accessed | tf_op | source)
XLA Modules:
  0.0 280.7 jit_solution(9846839067928465222)
XLA Ops:
  7.4 5.0 %collective-permute-start.1 = (f32[2,20,2,128]{3,2,1,0:T(2,128)S(1)}, f32[2,20,2,128]{3,2,1,0:T(2,128)S(1)}, u32[]{:S(2)}, u32[]{:S(2)}) collective-permute-start(f32[2,20,2,128]{3,2,1,0:T(2,128)S(1)} %get-tuple-element.94), channel_id=1, source_target_pairs={{0,4},{4,8},{8,12},{1,5},{5,9},{9,13},{2,6},{6,10},{10,14},{3,7},{... | collective-permute-start | bytes 122888 | tf_op jit(solution)/shard_map/ppermute | solution.py:30
  15.6 4.7 %collective-permute-start.3 = (f32[2,20,20,2]{3,2,1,0:T(8,128)S(1)}, f32[2,20,20,2]{3,2,1,0:T(8,128)S(1)}, u32[]{:S(2)}, u32[]{:S(2)}) collective-permute-start(f32[2,20,20,2]{3,2,1,0:T(8,128)S(1)} %get-tuple-element.92), channel_id=1, source_target_pairs={{0,1},{1,2},{2,3},{4,5},{5,6},{6,7},{8,9},{9,10},{10,11},{12,13},{... | collective-permute-start | bytes 19208 | tf_op jit(solution)/shard_map/ppermute | solution.py:30
  20.3 8.7 %collective-permute-done.4 = f32[2,20,20,2]{3,2,1,0:T(8,128)S(1)} collective-permute-done((f32[2,20,20,2]{3,2,1,0:T(8,128)S(1)}, f32[2,20,20,2]{3,2,1,0:T(8,128)S(1)}, u32[]{:S(2)}, u32[]{:S(2)}) %collective-permute-start.4) | collective-permute-done | bytes 6432 | tf_op jit(solution)/shard_map/ppermute | solution.py:31
  37.7 5.1 %collective-permute-start.5 = (f32[16,3,128]{2,1,0:T(4,128)S(1)}, f32[16,3,128]{2,1,0:T(4,128)S(1)}, u32[]{:S(2)}, u32[]{:S(2)}) collective-permute-start(f32[16,3,128]{2,1,0:T(4,128)S(1)} %get-tuple-element.114), channel_id=1, source_target_pairs={{0,4},{4,8},{8,12},{1,5},{5,9},{9,13},{2,6},{6,10},{10,14},{3,7},{... | collective-permute-start | bytes 73736 | tf_op jit(solution)/shard_map/ppermute | solution.py:30
  42.8 3.0 %collective-permute-start.7 = (f32[1025]{0:T(1024)S(1)}, f32[1025]{0:T(1024)S(1)}, u32[]{:S(2)}, u32[]{:S(2)}) collective-permute-start(f32[1025]{0:T(1024)S(1)} %pad_maximum_fusion.28), channel_id=1, source_target_pairs={{0,4},{4,0},{8,12},{12,8},{1,5},{5,1},{9,13},{13,9},{2,6},{6,2},{1... | collective-permute-start | bytes 12308 | tf_op jit(solution)/shard_map/ppermute | solution.py:176
  49.1 5.0 %collective-permute-start.8 = (f32[16,22,3]{2,1,0:T(8,128)S(1)}, f32[16,22,3]{2,1,0:T(8,128)S(1)}, u32[]{:S(2)}, u32[]{:S(2)}) collective-permute-start(f32[16,22,3]{2,1,0:T(8,128)S(1)} %get-tuple-element.104), channel_id=1, source_target_pairs={{0,1},{1,2},{2,3},{4,5},{5,6},{6,7},{8,9},{9,10},{10,11},{12,13},{... | collective-permute-start | bytes 12680 | tf_op jit(solution)/shard_map/ppermute | solution.py:30
  57.8 4.5 %collective-permute-start.16 = (f32[4,1,16,130]{3,2,1,0:T(8,128)S(1)}, f32[4,1,16,130]{3,2,1,0:T(8,128)S(1)}, u32[]{:S(2)}, u32[]{:S(2)}) collective-permute-start(f32[4,1,16,130]{3,2,1,0:T(8,128)S(1)} %get-tuple-element.112), channel_id=1, source_target_pairs={{0,4},{4,8},{8,12},{1,5},{5,9},{9,13},{2,6},{6,10},{10,14},{3,7},{... | collective-permute-start | bytes 99848 | tf_op jit(solution)/shard_map/ppermute | solution.py:30
  66.2 4.7 %collective-permute-start.18 = (f32[4,4,1,130]{3,2,1,0:T(1,128)S(1)}, f32[4,4,1,130]{3,2,1,0:T(1,128)S(1)}, u32[]{:S(2)}, u32[]{:S(2)}) collective-permute-start(f32[4,4,1,130]{3,2,1,0:T(1,128)S(1)} %get-tuple-element.96), channel_id=1, source_target_pairs={{0,1},{1,2},{2,3},{4,5},{5,6},{6,7},{8,9},{9,10},{10,11},{12,13},{... | collective-permute-start | bytes 24968 | tf_op jit(solution)/shard_map/ppermute | solution.py:30
  91.2 4.6 %collective-permute-start.20 = (f32[16,3,128]{2,1,0:T(4,128)S(1)}, f32[16,3,128]{2,1,0:T(4,128)S(1)}, u32[]{:S(2)}, u32[]{:S(2)}) collective-permute-start(f32[16,3,128]{2,1,0:T(4,128)S(1)} %get-tuple-element.110), channel_id=1, source_target_pairs={{0,4},{4,8},{8,12},{1,5},{5,9},{9,13},{2,6},{6,10},{10,14},{3,7},{... | collective-permute-start | bytes 73736 | tf_op jit(solution)/shard_map/ppermute | solution.py:30
  95.7 2.8 %collective-permute-start.22 = (f32[1026]{0:T(1024)S(1)}, f32[1026]{0:T(1024)S(1)}, u32[]{:S(2)}, u32[]{:S(2)}) collective-permute-start(f32[1026]{0:T(1024)S(1)} %concatenate.80), channel_id=1, source_target_pairs={{0,4},{4,0},{8,12},{12,8},{1,5},{5,1},{9,13},{13,9},{2,6},{6,2},{1... | collective-permute-start | bytes 12320 | tf_op jit(solution)/shard_map/ppermute | solution.py:176
  103.5 4.8 %collective-permute-start.23 = (f32[16,22,3]{2,1,0:T(8,128)S(1)}, f32[16,22,3]{2,1,0:T(8,128)S(1)}, u32[]{:S(2)}, u32[]{:S(2)}) collective-permute-start(f32[16,22,3]{2,1,0:T(8,128)S(1)} %get-tuple-element.102), channel_id=1, source_target_pairs={{0,1},{1,2},{2,3},{4,5},{5,6},{6,7},{8,9},{9,10},{10,11},{12,13},{... | collective-permute-start | bytes 12680 | tf_op jit(solution)/shard_map/ppermute | solution.py:30
  116.6 3.4 %collective-permute-start.28 = (f32[1026]{0:T(1024)S(1)}, f32[1026]{0:T(1024)S(1)}, u32[]{:S(2)}, u32[]{:S(2)}) collective-permute-start(f32[1026]{0:T(1024)S(1)} %add.542), channel_id=1, source_target_pairs={{0,2},{1,3},{2,0},{3,1},{4,6},{5,7},{6,4},{7,5},{8,10},{9,11},{10,... | collective-permute-start | bytes 12320 | tf_op jit(solution)/shard_map/ppermute | solution.py:176
  138.2 3.2 %collective-permute-done.31 = f32[3]{0:T(128)S(1)} collective-permute-done((f32[3]{0:T(128)S(1)}, f32[3]{0:T(128)S(1)}, u32[]{:S(2)}, u32[]{:S(2)}) %collective-permute-start.31) | collective-permute-done | bytes 44 | tf_op jit(solution)/shard_map/ppermute | solution.py:176
  142.0 3.0 %collective-permute-done.32 = f32[3]{0:T(128)S(1)} collective-permute-done((f32[3]{0:T(128)S(1)}, f32[3]{0:T(128)S(1)}, u32[]{:S(2)}, u32[]{:S(2)}) %collective-permute-start.32) | collective-permute-done | bytes 44 | tf_op jit(solution)/shard_map/ppermute | solution.py:176
  148.5 2.9 %collective-permute-start.34 = (f32[3]{0:T(128)S(1)}, f32[3]{0:T(128)S(1)}, u32[]{:S(2)}, u32[]{:S(2)}) collective-permute-start(f32[3]{0:T(128)S(1)} %add.554), channel_id=1, source_target_pairs={{0,2},{1,3},{2,0},{3,1},{4,6},{5,7},{6,4},{7,5},{8,10},{9,11},{10,... | collective-permute-start | bytes 44 | tf_op jit(solution)/shard_map/ppermute | solution.py:176
  167.8 4.5 %collective-permute-start.35 = (f32[16,3,128]{2,1,0:T(4,128)S(1)}, f32[16,3,128]{2,1,0:T(4,128)S(1)}, u32[]{:S(2)}, u32[]{:S(2)}) collective-permute-start(f32[16,3,128]{2,1,0:T(4,128)S(1)} %get-tuple-element.108), channel_id=1, source_target_pairs={{0,4},{4,8},{8,12},{1,5},{5,9},{9,13},{2,6},{6,10},{10,14},{3,7},{... | collective-permute-start | bytes 73736 | tf_op jit(solution)/shard_map/ppermute | solution.py:30
  178.5 4.8 %collective-permute-start.38 = (f32[16,22,3]{2,1,0:T(8,128)S(1)}, f32[16,22,3]{2,1,0:T(8,128)S(1)}, u32[]{:S(2)}, u32[]{:S(2)}) collective-permute-start(f32[16,22,3]{2,1,0:T(8,128)S(1)} %get-tuple-element.100), channel_id=1, source_target_pairs={{0,1},{1,2},{2,3},{4,5},{5,6},{6,7},{8,9},{9,10},{10,11},{12,13},{... | collective-permute-start | bytes 12680 | tf_op jit(solution)/shard_map/ppermute | solution.py:30
  191.6 3.1 %collective-permute-start.43 = (f32[1025]{0:T(1024)S(1)}, f32[1025]{0:T(1024)S(1)}, u32[]{:S(2)}, u32[]{:S(2)}) collective-permute-start(f32[1025]{0:T(1024)S(1)} %add.563), channel_id=1, source_target_pairs={{0,2},{1,3},{2,0},{3,1},{4,6},{5,7},{6,4},{7,5},{8,10},{9,11},{10,... | collective-permute-start | bytes 12308 | tf_op jit(solution)/shard_map/ppermute | solution.py:176
  211.2 4.5 %collective-permute-start.45 = (f32[16,3,128]{2,1,0:T(4,128)S(1)}, f32[16,3,128]{2,1,0:T(4,128)S(1)}, u32[]{:S(2)}, u32[]{:S(2)}) collective-permute-start(f32[16,3,128]{2,1,0:T(4,128)S(1)} %get-tuple-element.106), channel_id=1, source_target_pairs={{0,4},{4,8},{8,12},{1,5},{5,9},{9,13},{2,6},{6,10},{10,14},{3,7},{... | collective-permute-start | bytes 73736 | tf_op jit(solution)/shard_map/ppermute | solution.py:30
  222.2 4.5 %collective-permute-start.48 = (f32[16,22,3]{2,1,0:T(8,128)S(1)}, f32[16,22,3]{2,1,0:T(8,128)S(1)}, u32[]{:S(2)}, u32[]{:S(2)}) collective-permute-start(f32[16,22,3]{2,1,0:T(8,128)S(1)} %get-tuple-element.98), channel_id=1, source_target_pairs={{0,1},{1,2},{2,3},{4,5},{5,6},{6,7},{8,9},{9,10},{10,11},{12,13},{... | collective-permute-start | bytes 12680 | tf_op jit(solution)/shard_map/ppermute | solution.py:30
  235.3 3.3 %collective-permute-start.53 = (f32[1026]{0:T(1024)S(1)}, f32[1026]{0:T(1024)S(1)}, u32[]{:S(2)}, u32[]{:S(2)}) collective-permute-start(f32[1026]{0:T(1024)S(1)} %add.574), channel_id=1, source_target_pairs={{0,2},{1,3},{2,0},{3,1},{4,6},{5,7},{6,4},{7,5},{8,10},{9,11},{10,... | collective-permute-start | bytes 12320 | tf_op jit(solution)/shard_map/ppermute | solution.py:176
  256.7 3.3 %collective-permute-done.56 = f32[3]{0:T(128)S(1)} collective-permute-done((f32[3]{0:T(128)S(1)}, f32[3]{0:T(128)S(1)}, u32[]{:S(2)}, u32[]{:S(2)}) %collective-permute-start.56) | collective-permute-done | bytes 44 | tf_op jit(solution)/shard_map/ppermute | solution.py:176
  260.8 2.7 collective-permute-done.57
  267.1 2.9 %collective-permute-start.59 = (f32[3]{0:T(128)S(1)}, f32[3]{0:T(128)S(1)}, u32[]{:S(2)}, u32[]{:S(2)}) collective-permute-start(f32[3]{0:T(128)S(1)} %add.586), channel_id=1, source_target_pairs={{0,2},{1,3},{2,0},{3,1},{4,6},{5,7},{6,4},{7,5},{8,10},{9,11},{10,... | collective-permute-start | bytes 44 | tf_op jit(solution)/shard_map/ppermute | solution.py:176
  (375 shorter events, 160.4 us)
Async XLA Ops:
  2.7 17.6 %collective-permute-start.15 = (f32[1,2,16,130]{3,2,1,0:T(8,128)S(1)}, f32[1,2,16,130]{3,2,1,0:T(8,128)S(1)}, u32[]{:S(2)}, u32[]{:S(2)}) collective-permute-start(f32[1,2,16,130]{3,2,1,0:T(8,128)S(1)} %fusion.71), channel_id=1, source_target_pairs={{0,16},{16,0},{1,17},{17,1},{2,18},{18,2},{3,19},{19,3},{4,20},{20... | collective-permute-start | bytes 49928 | tf_op jit(solution)/shard_map/ppermute | solution.py:23
  14.3 14.7 %collective-permute-start.4 = (f32[2,20,20,2]{3,2,1,0:T(8,128)S(1)}, f32[2,20,20,2]{3,2,1,0:T(8,128)S(1)}, u32[]{:S(2)}, u32[]{:S(2)}) collective-permute-start(f32[2,20,20,2]{3,2,1,0:T(8,128)S(1)} %get-tuple-element.93), channel_id=1, source_target_pairs={{1,0},{2,1},{3,2},{5,4},{6,5},{7,6},{9,8},{10,9},{11,10},{13,12},{... | collective-permute-start | bytes 19208 | tf_op jit(solution)/shard_map/ppermute | solution.py:31
  15.6 14.6 %collective-permute-start.3 = (f32[2,20,20,2]{3,2,1,0:T(8,128)S(1)}, f32[2,20,20,2]{3,2,1,0:T(8,128)S(1)}, u32[]{:S(2)}, u32[]{:S(2)}) collective-permute-start(f32[2,20,20,2]{3,2,1,0:T(8,128)S(1)} %get-tuple-element.92), channel_id=1, source_target_pairs={{0,1},{1,2},{2,3},{4,5},{5,6},{6,7},{8,9},{9,10},{10,11},{12,13},{... | collective-permute-start | bytes 19208 | tf_op jit(solution)/shard_map/ppermute | solution.py:30
  36.4 11.3 %collective-permute-start.6 = (f32[16,3,128]{2,1,0:T(4,128)S(1)}, f32[16,3,128]{2,1,0:T(4,128)S(1)}, u32[]{:S(2)}, u32[]{:S(2)}) collective-permute-start(f32[16,3,128]{2,1,0:T(4,128)S(1)} %get-tuple-element.115), channel_id=1, source_target_pairs={{4,0},{8,4},{12,8},{5,1},{9,5},{13,9},{6,2},{10,6},{14,10},{7,3},{... | collective-permute-start | bytes 73736 | tf_op jit(solution)/shard_map/ppermute | solution.py:31
  37.7 10.0 %collective-permute-start.5 = (f32[16,3,128]{2,1,0:T(4,128)S(1)}, f32[16,3,128]{2,1,0:T(4,128)S(1)}, u32[]{:S(2)}, u32[]{:S(2)}) collective-permute-start(f32[16,3,128]{2,1,0:T(4,128)S(1)} %get-tuple-element.114), channel_id=1, source_target_pairs={{0,4},{4,8},{8,12},{1,5},{5,9},{9,13},{2,6},{6,10},{10,14},{3,7},{... | collective-permute-start | bytes 73736 | tf_op jit(solution)/shard_map/ppermute | solution.py:30
  47.8 14.6 %collective-permute-start.9 = (f32[16,22,3]{2,1,0:T(8,128)S(1)}, f32[16,22,3]{2,1,0:T(8,128)S(1)}, u32[]{:S(2)}, u32[]{:S(2)}) collective-permute-start(f32[16,22,3]{2,1,0:T(8,128)S(1)} %get-tuple-element.105), channel_id=1, source_target_pairs={{1,0},{2,1},{3,2},{5,4},{6,5},{7,6},{9,8},{10,9},{11,10},{13,12},{... | collective-permute-start | bytes 12680 | tf_op jit(solution)/shard_map/ppermute | solution.py:31
  49.1 13.3 %collective-permute-start.8 = (f32[16,22,3]{2,1,0:T(8,128)S(1)}, f32[16,22,3]{2,1,0:T(8,128)S(1)}, u32[]{:S(2)}, u32[]{:S(2)}) collective-permute-start(f32[16,22,3]{2,1,0:T(8,128)S(1)} %get-tuple-element.104), channel_id=1, source_target_pairs={{0,1},{1,2},{2,3},{4,5},{5,6},{6,7},{8,9},{9,10},{10,11},{12,13},{... | collective-permute-start | bytes 12680 | tf_op jit(solution)/shard_map/ppermute | solution.py:30
  54.1 8.2 %collective-permute-start.10 = (f32[1025]{0:T(1024)S(1)}, f32[1025]{0:T(1024)S(1)}, u32[]{:S(2)}, u32[]{:S(2)}) collective-permute-start(f32[1025]{0:T(1024)S(1)} %add.517), channel_id=1, source_target_pairs={{0,8},{4,12},{8,0},{12,4},{1,9},{5,13},{9,1},{13,5},{2,10},{6,14},... | collective-permute-start | bytes 12308 | tf_op jit(solution)/shard_map/ppermute | solution.py:176
  56.5 8.3 %collective-permute-start.17 = (f32[4,1,16,130]{3,2,1,0:T(8,128)S(1)}, f32[4,1,16,130]{3,2,1,0:T(8,128)S(1)}, u32[]{:S(2)}, u32[]{:S(2)}) collective-permute-start(f32[4,1,16,130]{3,2,1,0:T(8,128)S(1)} %get-tuple-element.113), channel_id=1, source_target_pairs={{4,0},{8,4},{12,8},{5,1},{9,5},{13,9},{6,2},{10,6},{14,10},{7,3},{... | collective-permute-start | bytes 99848 | tf_op jit(solution)/shard_map/ppermute | solution.py:31
  62.7 8.3 %collective-permute-start.11 = (f32[3,22,134]{2,1,0:T(8,128)S(1)}, f32[3,22,134]{2,1,0:T(8,128)S(1)}, u32[]{:S(2)}, u32[]{:S(2)}) collective-permute-start(f32[3,22,134]{2,1,0:T(8,128)S(1)} %slice_select_fusion.3), channel_id=1, source_target_pairs={{0,16},{16,0},{1,17},{17,1},{2,18},{18,2},{3,19},{19,3},{4,20},{20... | collective-permute-start | bytes 106136 | tf_op jit(solution)/shard_map/ppermute | solution.py:23
  62.8 8.1 %collective-permute-start.12 = (f32[1025]{0:T(1024)S(1)}, f32[1025]{0:T(1024)S(1)}, u32[]{:S(2)}, u32[]{:S(2)}) collective-permute-start(f32[1025]{0:T(1024)S(1)} %add.518), channel_id=1, source_target_pairs={{0,1},{1,0},{2,3},{3,2},{4,5},{5,4},{6,7},{7,6},{8,9},{9,8},{10,11... | collective-permute-start | bytes 12308 | tf_op jit(solution)/shard_map/ppermute | solution.py:176
  64.9 10.8 %collective-permute-start.19 = (f32[4,4,1,130]{3,2,1,0:T(1,128)S(1)}, f32[4,4,1,130]{3,2,1,0:T(1,128)S(1)}, u32[]{:S(2)}, u32[]{:S(2)}) collective-permute-start(f32[4,4,1,130]{3,2,1,0:T(1,128)S(1)} %get-tuple-element.97), channel_id=1, source_target_pairs={{1,0},{2,1},{3,2},{5,4},{6,5},{7,6},{9,8},{10,9},{11,10},{13,12},{... | collective-permute-start | bytes 24968 | tf_op jit(solution)/shard_map/ppermute | solution.py:31
  66.2 9.5 %collective-permute-start.18 = (f32[4,4,1,130]{3,2,1,0:T(1,128)S(1)}, f32[4,4,1,130]{3,2,1,0:T(1,128)S(1)}, u32[]{:S(2)}, u32[]{:S(2)}) collective-permute-start(f32[4,4,1,130]{3,2,1,0:T(1,128)S(1)} %get-tuple-element.96), channel_id=1, source_target_pairs={{0,1},{1,2},{2,3},{4,5},{5,6},{6,7},{8,9},{9,10},{10,11},{12,13},{... | collective-permute-start | bytes 24968 | tf_op jit(solution)/shard_map/ppermute | solution.py:30
  89.9 10.6 %collective-permute-start.21 = (f32[16,3,128]{2,1,0:T(4,128)S(1)}, f32[16,3,128]{2,1,0:T(4,128)S(1)}, u32[]{:S(2)}, u32[]{:S(2)}) collective-permute-start(f32[16,3,128]{2,1,0:T(4,128)S(1)} %get-tuple-element.111), channel_id=1, source_target_pairs={{4,0},{8,4},{12,8},{5,1},{9,5},{13,9},{6,2},{10,6},{14,10},{7,3},{... | collective-permute-start | bytes 73736 | tf_op jit(solution)/shard_map/ppermute | solution.py:31
  91.2 9.3 %collective-permute-start.20 = (f32[16,3,128]{2,1,0:T(4,128)S(1)}, f32[16,3,128]{2,1,0:T(4,128)S(1)}, u32[]{:S(2)}, u32[]{:S(2)}) collective-permute-start(f32[16,3,128]{2,1,0:T(4,128)S(1)} %get-tuple-element.110), channel_id=1, source_target_pairs={{0,4},{4,8},{8,12},{1,5},{5,9},{9,13},{2,6},{6,10},{10,14},{3,7},{... | collective-permute-start | bytes 73736 | tf_op jit(solution)/shard_map/ppermute | solution.py:30
  100.6 7.9 %collective-permute-start.24 = (f32[16,22,3]{2,1,0:T(8,128)S(1)}, f32[16,22,3]{2,1,0:T(8,128)S(1)}, u32[]{:S(2)}, u32[]{:S(2)}) collective-permute-start(f32[16,22,3]{2,1,0:T(8,128)S(1)} %get-tuple-element.103), channel_id=1, source_target_pairs={{1,0},{2,1},{3,2},{5,4},{6,5},{7,6},{9,8},{10,9},{11,10},{13,12},{... | collective-permute-start | bytes 12680 | tf_op jit(solution)/shard_map/ppermute | solution.py:31
  103.5 7.7 %collective-permute-start.23 = (f32[16,22,3]{2,1,0:T(8,128)S(1)}, f32[16,22,3]{2,1,0:T(8,128)S(1)}, u32[]{:S(2)}, u32[]{:S(2)}) collective-permute-start(f32[16,22,3]{2,1,0:T(8,128)S(1)} %get-tuple-element.102), channel_id=1, source_target_pairs={{0,1},{1,2},{2,3},{4,5},{5,6},{6,7},{8,9},{9,10},{10,11},{12,13},{... | collective-permute-start | bytes 12680 | tf_op jit(solution)/shard_map/ppermute | solution.py:30
  166.5 9.6 %collective-permute-start.36 = (f32[16,3,128]{2,1,0:T(4,128)S(1)}, f32[16,3,128]{2,1,0:T(4,128)S(1)}, u32[]{:S(2)}, u32[]{:S(2)}) collective-permute-start(f32[16,3,128]{2,1,0:T(4,128)S(1)} %get-tuple-element.109), channel_id=1, source_target_pairs={{4,0},{8,4},{12,8},{5,1},{9,5},{13,9},{6,2},{10,6},{14,10},{7,3},{... | collective-permute-start | bytes 73736 | tf_op jit(solution)/shard_map/ppermute | solution.py:31
  167.8 8.3 %collective-permute-start.35 = (f32[16,3,128]{2,1,0:T(4,128)S(1)}, f32[16,3,128]{2,1,0:T(4,128)S(1)}, u32[]{:S(2)}, u32[]{:S(2)}) collective-permute-start(f32[16,3,128]{2,1,0:T(4,128)S(1)} %get-tuple-element.108), channel_id=1, source_target_pairs={{0,4},{4,8},{8,12},{1,5},{5,9},{9,13},{2,6},{6,10},{10,14},{3,7},{... | collective-permute-start | bytes 73736 | tf_op jit(solution)/shard_map/ppermute | solution.py:30
  176.3 7.6 %collective-permute-start.39 = (f32[16,22,3]{2,1,0:T(8,128)S(1)}, f32[16,22,3]{2,1,0:T(8,128)S(1)}, u32[]{:S(2)}, u32[]{:S(2)}) collective-permute-start(f32[16,22,3]{2,1,0:T(8,128)S(1)} %get-tuple-element.101), channel_id=1, source_target_pairs={{1,0},{2,1},{3,2},{5,4},{6,5},{7,6},{9,8},{10,9},{11,10},{13,12},{... | collective-permute-start | bytes 12680 | tf_op jit(solution)/shard_map/ppermute | solution.py:31
  178.5 7.7 %collective-permute-start.38 = (f32[16,22,3]{2,1,0:T(8,128)S(1)}, f32[16,22,3]{2,1,0:T(8,128)S(1)}, u32[]{:S(2)}, u32[]{:S(2)}) collective-permute-start(f32[16,22,3]{2,1,0:T(8,128)S(1)} %get-tuple-element.100), channel_id=1, source_target_pairs={{0,1},{1,2},{2,3},{4,5},{5,6},{6,7},{8,9},{9,10},{10,11},{12,13},{... | collective-permute-start | bytes 12680 | tf_op jit(solution)/shard_map/ppermute | solution.py:30
  209.9 9.6 %collective-permute-start.46 = (f32[16,3,128]{2,1,0:T(4,128)S(1)}, f32[16,3,128]{2,1,0:T(4,128)S(1)}, u32[]{:S(2)}, u32[]{:S(2)}) collective-permute-start(f32[16,3,128]{2,1,0:T(4,128)S(1)} %get-tuple-element.107), channel_id=1, source_target_pairs={{4,0},{8,4},{12,8},{5,1},{9,5},{13,9},{6,2},{10,6},{14,10},{7,3},{... | collective-permute-start | bytes 73736 | tf_op jit(solution)/shard_map/ppermute | solution.py:31
  211.2 8.3 %collective-permute-start.45 = (f32[16,3,128]{2,1,0:T(4,128)S(1)}, f32[16,3,128]{2,1,0:T(4,128)S(1)}, u32[]{:S(2)}, u32[]{:S(2)}) collective-permute-start(f32[16,3,128]{2,1,0:T(4,128)S(1)} %get-tuple-element.106), channel_id=1, source_target_pairs={{0,4},{4,8},{8,12},{1,5},{5,9},{9,13},{2,6},{6,10},{10,14},{3,7},{... | collective-permute-start | bytes 73736 | tf_op jit(solution)/shard_map/ppermute | solution.py:30
  222.2 7.7 %collective-permute-start.48 = (f32[16,22,3]{2,1,0:T(8,128)S(1)}, f32[16,22,3]{2,1,0:T(8,128)S(1)}, u32[]{:S(2)}, u32[]{:S(2)}) collective-permute-start(f32[16,22,3]{2,1,0:T(8,128)S(1)} %get-tuple-element.98), channel_id=1, source_target_pairs={{0,1},{1,2},{2,3},{4,5},{5,6},{6,7},{8,9},{9,10},{10,11},{12,13},{... | collective-permute-start | bytes 12680 | tf_op jit(solution)/shard_map/ppermute | solution.py:30
  (62 other events, 292.4 us)

commit v3 on v2

--- a/solution.py
+++ b/solution.py
@@ -170,12 +170,20 @@
         if size & (size - 1):
             stages.append(lambda value, axis=axis: lax.psum(value, axis))
             continue
+        if size == 4:
+            stages.append(functools.partial(sum_of_four, axis=axis))
+            continue
         step = 1
         while step < size:
             pairs = [(i, i ^ step) for i in range(size)]
             stages.append(lambda value, axis=axis, pairs=pairs: value + lax.ppermute(value, axis, pairs))
             step *= 2
     return stages
+
+
+def sum_of_four(value, axis):
+    got = [value] + [lax.ppermute(value, axis, [(i, i ^ s) for i in range(4)]) for s in (1, 2, 3)]
+    return (got[0] + got[1]) + (got[2] + got[3])
 
 
 def butterfly(value, axes):

time: 282 us -> 279 us (0.989)
  waiting for transfers between devices: 63.8 us -> 49.1 us
  starting transfers between devices: 121 us -> 129 us
  local copies, waits for them, and re-layouts: 17.9 us -> 21.7 us
    ppermute x0 -> x36, starting transfers between devices: none -> 58.4 us  [sum_of_four(): lax.ppermute(value, axis, [(i, i ^ s) for i in range(4)])]
    ppermute x26 -> x2, starting transfers between devices: 48 us -> 0.33 us  [butterfly_stages(): lax.ppermute(value, axis, pairs)]
    ppermute x26 -> x2, waiting for transfers between devices: 41.3 us -> 1.92 us  [butterfly_stages(): lax.ppermute(value, axis, pairs)]
    ppermute x0 -> x36, waiting for transfers between devices: none -> 18.6 us  [sum_of_four(): lax.ppermute(value, axis, [(i, i ^ s) for i in range(4)])]
    ppermute x12, waiting for transfers between devices: 9.67 us -> 14.7 us  [pad_side(): before = lax.ppermute(last, axis, up)]
    div x4 -> x0, other arithmetic: 4.11 us -> none  [the longest x2 3.97 us: body(): (wide_local + coarse_on_rim(wholes) - first_proj * wide_zed) / first_len]
    ppermute x12, starting transfers between devices: 56.9 us -> 52.9 us  [pad_side(): before = lax.ppermute(last, axis, up)]
    ppermute x6, waiting for transfers between devices: 0.02 us -> 3.77 us  [pad_side(): got = lax.ppermute(jnp.where(first, last, leading), axis, [(0, 1), (1, 0)])]
  transfers between devices with their start and end apart: 60 -> 72, of which waited for: 33 -> 35; matrix products, arithmetic and copies ran while one was open for 2% -> 5% of each run, Pallas kernels for 0% -> 0%
where the time goes in v3:
time: 279 us; the launch traced here: 277 us
  starting transfers between devices  129 us (46%)
  waiting for transfers between devices  49.1 us (18%)
  other arithmetic  30.8 us (11%)
  matrix products  25.4 us (9%)
  local copies, waits for them, and re-layouts  21.7 us (8%)
  between operations  21 us (8%)
    ppermute x36, starting transfers between devices, sum_of_four(): lax.ppermute(value, axis, [(i, i ^ s) for i in range(4)])  58.4 us
    ppermute x12, starting transfers between devices, pad_side(): before = lax.ppermute(last, axis, up)  52.9 us
    ppermute x36, waiting for transfers between devices, sum_of_four(): lax.ppermute(value, axis, [(i, i ^ s) for i in range(4)])  18.6 us
    ppermute x12, starting transfers between devices, pad_side(): after = lax.ppermute(leading, axis, down)  15.5 us
    ppermute x12, waiting for transfers between devices, pad_side(): before = lax.ppermute(last, axis, up)  14.7 us
    unnamed x72, local copies, waits for them, and re-layouts  8.85 us
    ppermute x12, waiting for transfers between devices, pad_side(): after = lax.ppermute(leading, axis, down)  7.85 us
  transfers between devices with their start and end apart: 72, of which 35 were waited for; matrix products, arithmetic and copies ran while one was open for 5% of the time, Pallas kernels for 0%

profile of v3, /device:TPU:0, one launch (start us, length us, event | category | flops | bytes accessed | tf_op | source)
XLA Modules:
  0.0 276.8 jit_solution(10311138524129555078)
XLA Ops:
  10.0 5.0 %collective-permute-start.1 = (f32[2,20,2,128]{3,2,1,0:T(2,128)S(1)}, f32[2,20,2,128]{3,2,1,0:T(2,128)S(1)}, u32[]{:S(2)}, u32[]{:S(2)}) collective-permute-start(f32[2,20,2,128]{3,2,1,0:T(2,128)S(1)} %get-tuple-element.78), channel_id=1, source_target_pairs={{0,4},{4,8},{8,12},{1,5},{5,9},{9,13},{2,6},{6,10},{10,14},{3,7},{... | collective-permute-start | bytes 122888 | tf_op jit(solution)/shard_map/ppermute | solution.py:30
  18.3 4.7 %collective-permute-start.3 = (f32[2,20,20,2]{3,2,1,0:T(8,128)S(1)}, f32[2,20,20,2]{3,2,1,0:T(8,128)S(1)}, u32[]{:S(2)}, u32[]{:S(2)}) collective-permute-start(f32[2,20,20,2]{3,2,1,0:T(8,128)S(1)} %get-tuple-element.76), channel_id=1, source_target_pairs={{0,1},{1,2},{2,3},{4,5},{5,6},{6,7},{8,9},{9,10},{10,11},{12,13},{... | collective-permute-start | bytes 19208 | tf_op jit(solution)/shard_map/ppermute | solution.py:30
  24.9 5.4 %collective-permute-start.18 = (f32[4,1,16,130]{3,2,1,0:T(8,128)}, f32[4,1,16,130]{3,2,1,0:T(8,128)S(1)}, u32[]{:S(2)}, u32[]{:S(2)}) collective-permute-start(f32[4,1,16,130]{3,2,1,0:T(8,128)} %get-tuple-element.96), channel_id=1, source_target_pairs={{0,4},{4,8},{8,12},{1,5},{5,9},{9,13},{2,6},{6,10},{10,14},{3,7},{... | collective-permute-start | bytes 99848 | tf_op jit(solution)/shard_map/ppermute | solution.py:30
  39.8 4.1 %collective-permute-start.8 = (f32[1025]{0:T(1024)S(1)}, f32[1025]{0:T(1024)S(1)}, u32[]{:S(2)}, u32[]{:S(2)}) collective-permute-start(f32[1025]{0:T(1024)S(1)} %pad_maximum_fusion.28), channel_id=1, source_target_pairs={{0,8},{4,12},{8,0},{12,4},{1,9},{5,13},{9,1},{13,5},{2,10},{6,14},... | collective-permute-start | bytes 12308 | tf_op jit(solution)/shard_map/ppermute | solution.py:185
  48.5 2.8 %collective-permute-start.5 = (f32[16,3,128]{2,1,0:T(4,128)S(1)}, f32[16,3,128]{2,1,0:T(4,128)S(1)}, u32[]{:S(2)}, u32[]{:S(2)}) collective-permute-start(f32[16,3,128]{2,1,0:T(4,128)S(1)} %get-tuple-element.98), channel_id=1, source_target_pairs={{0,4},{4,8},{8,12},{1,5},{5,9},{9,13},{2,6},{6,10},{10,14},{3,7},{... | collective-permute-start | bytes 73736 | tf_op jit(solution)/shard_map/ppermute | solution.py:30
  53.0 3.6 %collective-permute-start.13 = (f32[1025]{0:T(1024)S(1)}, f32[1025]{0:T(1024)S(1)}, u32[]{:S(2)}, u32[]{:S(2)}) collective-permute-start(f32[1025]{0:T(1024)S(1)} %add_add_fusion.7), channel_id=1, source_target_pairs={{0,2},{1,3},{2,0},{3,1},{4,6},{5,7},{6,4},{7,5},{8,10},{9,11},{10,... | collective-permute-start | bytes 12308 | tf_op jit(solution)/shard_map/ppermute | solution.py:185
  69.0 5.2 %collective-permute-start.20 = (f32[4,4,1,130]{3,2,1,0:T(1,128)S(1)}, f32[4,4,1,130]{3,2,1,0:T(1,128)S(1)}, u32[]{:S(2)}, u32[]{:S(2)}) collective-permute-start(f32[4,4,1,130]{3,2,1,0:T(1,128)S(1)} %get-tuple-element.80), channel_id=1, source_target_pairs={{0,1},{1,2},{2,3},{4,5},{5,6},{6,7},{8,9},{9,10},{10,11},{12,13},{... | collective-permute-start | bytes 24968 | tf_op jit(solution)/shard_map/ppermute | solution.py:30
  89.9 3.2 %collective-permute-start.25 = (f32[1026]{0:T(1024)S(1)}, f32[1026]{0:T(1024)S(1)}, u32[]{:S(2)}, u32[]{:S(2)}) collective-permute-start(f32[1026]{0:T(1024)S(1)} %concatenate.80), channel_id=1, source_target_pairs={{0,8},{4,12},{8,0},{12,4},{1,9},{5,13},{9,1},{13,5},{2,10},{6,14},... | collective-permute-start | bytes 12320 | tf_op jit(solution)/shard_map/ppermute | solution.py:185
  96.0 4.5 %collective-permute-start.22 = (f32[16,3,128]{2,1,0:T(4,128)S(1)}, f32[16,3,128]{2,1,0:T(4,128)S(1)}, u32[]{:S(2)}, u32[]{:S(2)}) collective-permute-start(f32[16,3,128]{2,1,0:T(4,128)S(1)} %get-tuple-element.94), channel_id=1, source_target_pairs={{0,4},{4,8},{8,12},{1,5},{5,9},{9,13},{2,6},{6,10},{10,14},{3,7},{... | collective-permute-start | bytes 73736 | tf_op jit(solution)/shard_map/ppermute | solution.py:30
  102.1 3.8 %collective-permute-start.30 = (f32[1026]{0:T(1024)S(1)}, f32[1026]{0:T(1024)S(1)}, u32[]{:S(2)}, u32[]{:S(2)}) collective-permute-start(f32[1026]{0:T(1024)S(1)} %add_add_fusion.5), channel_id=1, source_target_pairs={{0,2},{1,3},{2,0},{3,1},{4,6},{5,7},{6,4},{7,5},{8,10},{9,11},{10,... | collective-permute-start | bytes 12320 | tf_op jit(solution)/shard_map/ppermute | solution.py:185
  109.3 4.8 %collective-permute-start.27 = (f32[16,22,3]{2,1,0:T(8,128)S(1)}, f32[16,22,3]{2,1,0:T(8,128)S(1)}, u32[]{:S(2)}, u32[]{:S(2)}) collective-permute-start(f32[16,22,3]{2,1,0:T(8,128)S(1)} %get-tuple-element.86), channel_id=1, source_target_pairs={{0,1},{1,2},{2,3},{4,5},{5,6},{6,7},{8,9},{9,10},{10,11},{12,13},{... | collective-permute-start | bytes 12680 | tf_op jit(solution)/shard_map/ppermute | solution.py:30
  134.9 3.8 %collective-permute-start.36 = (f32[3]{0:T(128)S(1)}, f32[3]{0:T(128)S(1)}, u32[]{:S(2)}, u32[]{:S(2)}) collective-permute-start(f32[3]{0:T(128)S(1)} %add.591), channel_id=1, source_target_pairs={{0,8},{4,12},{8,0},{12,4},{1,9},{5,13},{9,1},{13,5},{2,10},{6,14},... | collective-permute-start | bytes 44 | tf_op jit(solution)/shard_map/ppermute | solution.py:185
  140.2 2.9 %collective-permute-done.37 = f32[3]{0:T(128)S(1)} collective-permute-done((f32[3]{0:T(128)S(1)}, f32[3]{0:T(128)S(1)}, u32[]{:S(2)}, u32[]{:S(2)}) %collective-permute-start.37) | collective-permute-done | bytes 44 | tf_op jit(solution)/shard_map/ppermute | solution.py:185
  143.2 3.5 %collective-permute-start.39 = (f32[3]{0:T(128)S(1)}, f32[3]{0:T(128)S(1)}, u32[]{:S(2)}, u32[]{:S(2)}) collective-permute-start(f32[3]{0:T(128)S(1)} %add_add_fusion.11), channel_id=1, source_target_pairs={{0,2},{1,3},{2,0},{3,1},{4,6},{5,7},{6,4},{7,5},{8,10},{9,11},{10,... | collective-permute-start | bytes 44 | tf_op jit(solution)/shard_map/ppermute | solution.py:185
  148.2 3.8 %collective-permute-done.40 = f32[3]{0:T(128)S(1)} collective-permute-done((f32[3]{0:T(128)S(1)}, f32[3]{0:T(128)S(1)}, u32[]{:S(2)}, u32[]{:S(2)}) %collective-permute-start.40) | collective-permute-done | bytes 44 | tf_op jit(solution)/shard_map/ppermute | solution.py:185
  170.4 4.5 %collective-permute-start.41 = (f32[16,3,128]{2,1,0:T(4,128)S(1)}, f32[16,3,128]{2,1,0:T(4,128)S(1)}, u32[]{:S(2)}, u32[]{:S(2)}) collective-permute-start(f32[16,3,128]{2,1,0:T(4,128)S(1)} %get-tuple-element.92), channel_id=1, source_target_pairs={{0,4},{4,8},{8,12},{1,5},{5,9},{9,13},{2,6},{6,10},{10,14},{3,7},{... | collective-permute-start | bytes 73736 | tf_op jit(solution)/shard_map/ppermute | solution.py:30
  181.6 4.8 %collective-permute-start.46 = (f32[16,22,3]{2,1,0:T(8,128)S(1)}, f32[16,22,3]{2,1,0:T(8,128)S(1)}, u32[]{:S(2)}, u32[]{:S(2)}) collective-permute-start(f32[16,22,3]{2,1,0:T(8,128)S(1)} %get-tuple-element.84), channel_id=1, source_target_pairs={{0,1},{1,2},{2,3},{4,5},{5,6},{6,7},{8,9},{9,10},{10,11},{12,13},{... | collective-permute-start | bytes 12680 | tf_op jit(solution)/shard_map/ppermute | solution.py:30
  206.1 3.2 %collective-permute-start.56 = (f32[1026]{0:T(1024)S(1)}, f32[1026]{0:T(1024)S(1)}, u32[]{:S(2)}, u32[]{:S(2)}) collective-permute-start(f32[1026]{0:T(1024)S(1)} %concatenate.88), channel_id=1, source_target_pairs={{0,8},{4,12},{8,0},{12,4},{1,9},{5,13},{9,1},{13,5},{2,10},{6,14},... | collective-permute-start | bytes 12320 | tf_op jit(solution)/shard_map/ppermute | solution.py:185
  212.2 4.5 %collective-permute-start.53 = (f32[16,3,128]{2,1,0:T(4,128)S(1)}, f32[16,3,128]{2,1,0:T(4,128)S(1)}, u32[]{:S(2)}, u32[]{:S(2)}) collective-permute-start(f32[16,3,128]{2,1,0:T(4,128)S(1)} %get-tuple-element.90), channel_id=1, source_target_pairs={{0,4},{4,8},{8,12},{1,5},{5,9},{9,13},{2,6},{6,10},{10,14},{3,7},{... | collective-permute-start | bytes 73736 | tf_op jit(solution)/shard_map/ppermute | solution.py:30
  224.7 4.6 %collective-permute-start.58 = (f32[16,22,3]{2,1,0:T(8,128)S(1)}, f32[16,22,3]{2,1,0:T(8,128)S(1)}, u32[]{:S(2)}, u32[]{:S(2)}) collective-permute-start(f32[16,22,3]{2,1,0:T(8,128)S(1)} %get-tuple-element.82), channel_id=1, source_target_pairs={{0,1},{1,2},{2,3},{4,5},{5,6},{6,7},{8,9},{9,10},{10,11},{12,13},{... | collective-permute-start | bytes 12680 | tf_op jit(solution)/shard_map/ppermute | solution.py:30
  250.1 3.7 %collective-permute-start.67 = (f32[3]{0:T(128)S(1)}, f32[3]{0:T(128)S(1)}, u32[]{:S(2)}, u32[]{:S(2)}) collective-permute-start(f32[3]{0:T(128)S(1)} %add.629), channel_id=1, source_target_pairs={{0,8},{4,12},{8,0},{12,4},{1,9},{5,13},{9,1},{13,5},{2,10},{6,14},... | collective-permute-start | bytes 44 | tf_op jit(solution)/shard_map/ppermute | solution.py:185
  255.3 2.9 %collective-permute-done.68 = f32[3]{0:T(128)S(1)} collective-permute-done((f32[3]{0:T(128)S(1)}, f32[3]{0:T(128)S(1)}, u32[]{:S(2)}, u32[]{:S(2)}) %collective-permute-start.68) | collective-permute-done | bytes 44 | tf_op jit(solution)/shard_map/ppermute | solution.py:185
  258.2 4.0 %collective-permute-start.70 = (f32[3]{0:T(128)S(1)}, f32[3]{0:T(128)S(1)}, u32[]{:S(2)}, u32[]{:S(2)}) collective-permute-start(f32[3]{0:T(128)S(1)} %add_add_fusion.9), channel_id=1, source_target_pairs={{0,2},{1,3},{2,0},{3,1},{4,6},{5,7},{6,4},{7,5},{8,10},{9,11},{10,... | collective-permute-start | bytes 44 | tf_op jit(solution)/shard_map/ppermute | solution.py:185
  263.7 3.8 %collective-permute-done.71 = f32[3]{0:T(128)S(1)} collective-permute-done((f32[3]{0:T(128)S(1)}, f32[3]{0:T(128)S(1)}, u32[]{:S(2)}, u32[]{:S(2)}) %collective-permute-start.71) | collective-permute-done | bytes 44 | tf_op jit(solution)/shard_map/ppermute | solution.py:185
  (405 shorter events, 158.5 us)
Async XLA Ops:
  17.0 14.7 %collective-permute-start.4 = (f32[2,20,20,2]{3,2,1,0:T(8,128)S(1)}, f32[2,20,20,2]{3,2,1,0:T(8,128)S(1)}, u32[]{:S(2)}, u32[]{:S(2)}) collective-permute-start(f32[2,20,20,2]{3,2,1,0:T(8,128)S(1)} %get-tuple-element.77), channel_id=1, source_target_pairs={{1,0},{2,1},{3,2},{5,4},{6,5},{7,6},{9,8},{10,9},{11,10},{13,12},{... | collective-permute-start | bytes 19208 | tf_op jit(solution)/shard_map/ppermute | solution.py:31
  18.3 14.6 %collective-permute-start.3 = (f32[2,20,20,2]{3,2,1,0:T(8,128)S(1)}, f32[2,20,20,2]{3,2,1,0:T(8,128)S(1)}, u32[]{:S(2)}, u32[]{:S(2)}) collective-permute-start(f32[2,20,20,2]{3,2,1,0:T(8,128)S(1)} %get-tuple-element.76), channel_id=1, source_target_pairs={{0,1},{1,2},{2,3},{4,5},{5,6},{6,7},{8,9},{9,10},{10,11},{12,13},{... | collective-permute-start | bytes 19208 | tf_op jit(solution)/shard_map/ppermute | solution.py:30
  23.6 44.0 %collective-permute-start.19 = (f32[4,1,16,130]{3,2,1,0:T(8,128)}, f32[4,1,16,130]{3,2,1,0:T(8,128)S(1)}, u32[]{:S(2)}, u32[]{:S(2)}) collective-permute-start(f32[4,1,16,130]{3,2,1,0:T(8,128)} %get-tuple-element.97), channel_id=1, source_target_pairs={{4,0},{8,4},{12,8},{5,1},{9,5},{13,9},{6,2},{10,6},{14,10},{7,3},{... | collective-permute-start | bytes 99848 | tf_op jit(solution)/shard_map/ppermute | solution.py:31
  24.9 42.7 %collective-permute-start.18 = (f32[4,1,16,130]{3,2,1,0:T(8,128)}, f32[4,1,16,130]{3,2,1,0:T(8,128)S(1)}, u32[]{:S(2)}, u32[]{:S(2)}) collective-permute-start(f32[4,1,16,130]{3,2,1,0:T(8,128)} %get-tuple-element.96), channel_id=1, source_target_pairs={{0,4},{4,8},{8,12},{1,5},{5,9},{9,13},{2,6},{6,10},{10,14},{3,7},{... | collective-permute-start | bytes 99848 | tf_op jit(solution)/shard_map/ppermute | solution.py:30
  43.9 7.5 %collective-permute-start.7 = (f32[1025]{0:T(1024)S(1)}, f32[1025]{0:T(1024)S(1)}, u32[]{:S(2)}, u32[]{:S(2)}) collective-permute-start(f32[1025]{0:T(1024)S(1)} %pad_maximum_fusion.28), channel_id=1, source_target_pairs={{0,4},{4,0},{8,12},{12,8},{1,5},{5,1},{9,13},{13,9},{2,6},{6,2},{1... | collective-permute-start | bytes 12308 | tf_op jit(solution)/shard_map/ppermute | solution.py:185
  58.3 7.6 %collective-permute-start.11 = (f32[16,22,3]{2,1,0:T(8,128)S(1)}, f32[16,22,3]{2,1,0:T(8,128)S(1)}, u32[]{:S(2)}, u32[]{:S(2)}) collective-permute-start(f32[16,22,3]{2,1,0:T(8,128)S(1)} %get-tuple-element.89), channel_id=1, source_target_pairs={{1,0},{2,1},{3,2},{5,4},{6,5},{7,6},{9,8},{10,9},{11,10},{13,12},{... | collective-permute-start | bytes 12680 | tf_op jit(solution)/shard_map/ppermute | solution.py:31
  67.7 7.6 %collective-permute-start.21 = (f32[4,4,1,130]{3,2,1,0:T(1,128)S(1)}, f32[4,4,1,130]{3,2,1,0:T(1,128)S(1)}, u32[]{:S(2)}, u32[]{:S(2)}) collective-permute-start(f32[4,4,1,130]{3,2,1,0:T(1,128)S(1)} %get-tuple-element.81), channel_id=1, source_target_pairs={{1,0},{2,1},{3,2},{5,4},{6,5},{7,6},{9,8},{10,9},{11,10},{13,12},{... | collective-permute-start | bytes 24968 | tf_op jit(solution)/shard_map/ppermute | solution.py:31
  89.9 10.6 %collective-permute-start.25 = (f32[1026]{0:T(1024)S(1)}, f32[1026]{0:T(1024)S(1)}, u32[]{:S(2)}, u32[]{:S(2)}) collective-permute-start(f32[1026]{0:T(1024)S(1)} %concatenate.80), channel_id=1, source_target_pairs={{0,8},{4,12},{8,0},{12,4},{1,9},{5,13},{9,1},{13,5},{2,10},{6,14},... | collective-permute-start | bytes 12320 | tf_op jit(solution)/shard_map/ppermute | solution.py:185
  102.1 11.9 %collective-permute-start.30 = (f32[1026]{0:T(1024)S(1)}, f32[1026]{0:T(1024)S(1)}, u32[]{:S(2)}, u32[]{:S(2)}) collective-permute-start(f32[1026]{0:T(1024)S(1)} %add_add_fusion.5), channel_id=1, source_target_pairs={{0,2},{1,3},{2,0},{3,1},{4,6},{5,7},{6,4},{7,5},{8,10},{9,11},{10,... | collective-permute-start | bytes 12320 | tf_op jit(solution)/shard_map/ppermute | solution.py:185
  106.0 8.1 %collective-permute-start.31 = (f32[1026]{0:T(1024)S(1)}, f32[1026]{0:T(1024)S(1)}, u32[]{:S(2)}, u32[]{:S(2)}) collective-permute-start(f32[1026]{0:T(1024)S(1)} %add_add_fusion.5), channel_id=1, source_target_pairs={{0,3},{1,2},{2,1},{3,0},{4,7},{5,6},{6,5},{7,4},{8,11},{9,10},{10,... | collective-permute-start | bytes 12320 | tf_op jit(solution)/shard_map/ppermute | solution.py:185
  108.0 7.6 %collective-permute-start.28 = (f32[16,22,3]{2,1,0:T(8,128)S(1)}, f32[16,22,3]{2,1,0:T(8,128)S(1)}, u32[]{:S(2)}, u32[]{:S(2)}) collective-permute-start(f32[16,22,3]{2,1,0:T(8,128)S(1)} %get-tuple-element.87), channel_id=1, source_target_pairs={{1,0},{2,1},{3,2},{5,4},{6,5},{7,6},{9,8},{10,9},{11,10},{13,12},{... | collective-permute-start | bytes 12680 | tf_op jit(solution)/shard_map/ppermute | solution.py:31
  109.3 7.7 %collective-permute-start.27 = (f32[16,22,3]{2,1,0:T(8,128)S(1)}, f32[16,22,3]{2,1,0:T(8,128)S(1)}, u32[]{:S(2)}, u32[]{:S(2)}) collective-permute-start(f32[16,22,3]{2,1,0:T(8,128)S(1)} %get-tuple-element.86), channel_id=1, source_target_pairs={{0,1},{1,2},{2,3},{4,5},{5,6},{6,7},{8,9},{9,10},{10,11},{12,13},{... | collective-permute-start | bytes 12680 | tf_op jit(solution)/shard_map/ppermute | solution.py:30
  165.5 9.4 %collective-permute-start.44 = (f32[1025]{0:T(1024)S(1)}, f32[1025]{0:T(1024)S(1)}, u32[]{:S(2)}, u32[]{:S(2)}) collective-permute-start(f32[1025]{0:T(1024)S(1)} %pad_maximum_fusion.29), channel_id=1, source_target_pairs={{0,8},{4,12},{8,0},{12,4},{1,9},{5,13},{9,1},{13,5},{2,10},{6,14},... | collective-permute-start | bytes 12308 | tf_op jit(solution)/shard_map/ppermute | solution.py:185
  166.6 8.4 %collective-permute-start.45 = (f32[1025]{0:T(1024)S(1)}, f32[1025]{0:T(1024)S(1)}, u32[]{:S(2)}, u32[]{:S(2)}) collective-permute-start(f32[1025]{0:T(1024)S(1)} %pad_maximum_fusion.29), channel_id=1, source_target_pairs={{0,12},{4,8},{8,4},{12,0},{1,13},{5,9},{9,5},{13,1},{2,14},{6,10},... | collective-permute-start | bytes 12308 | tf_op jit(solution)/shard_map/ppermute | solution.py:185
  176.6 9.8 %collective-permute-start.49 = (f32[1025]{0:T(1024)S(1)}, f32[1025]{0:T(1024)S(1)}, u32[]{:S(2)}, u32[]{:S(2)}) collective-permute-start(f32[1025]{0:T(1024)S(1)} %add_add_fusion.3), channel_id=1, source_target_pairs={{0,2},{1,3},{2,0},{3,1},{4,6},{5,7},{6,4},{7,5},{8,10},{9,11},{10,... | collective-permute-start | bytes 12308 | tf_op jit(solution)/shard_map/ppermute | solution.py:185
  177.9 8.5 %collective-permute-start.50 = (f32[1025]{0:T(1024)S(1)}, f32[1025]{0:T(1024)S(1)}, u32[]{:S(2)}, u32[]{:S(2)}) collective-permute-start(f32[1025]{0:T(1024)S(1)} %add_add_fusion.3), channel_id=1, source_target_pairs={{0,3},{1,2},{2,1},{3,0},{4,7},{5,6},{6,5},{7,4},{8,11},{9,10},{10,... | collective-permute-start | bytes 12308 | tf_op jit(solution)/shard_map/ppermute | solution.py:185
  178.8 7.7 %collective-permute-start.48 = (f32[1025]{0:T(1024)S(1)}, f32[1025]{0:T(1024)S(1)}, u32[]{:S(2)}, u32[]{:S(2)}) collective-permute-start(f32[1025]{0:T(1024)S(1)} %add_add_fusion.3), channel_id=1, source_target_pairs={{0,1},{1,0},{2,3},{3,2},{4,5},{5,4},{6,7},{7,6},{8,9},{9,8},{10,11... | collective-permute-start | bytes 12308 | tf_op jit(solution)/shard_map/ppermute | solution.py:185
  180.3 7.6 %collective-permute-start.47 = (f32[16,22,3]{2,1,0:T(8,128)S(1)}, f32[16,22,3]{2,1,0:T(8,128)S(1)}, u32[]{:S(2)}, u32[]{:S(2)}) collective-permute-start(f32[16,22,3]{2,1,0:T(8,128)S(1)} %get-tuple-element.85), channel_id=1, source_target_pairs={{1,0},{2,1},{3,2},{5,4},{6,5},{7,6},{9,8},{10,9},{11,10},{13,12},{... | collective-permute-start | bytes 12680 | tf_op jit(solution)/shard_map/ppermute | solution.py:31
  181.6 7.7 %collective-permute-start.46 = (f32[16,22,3]{2,1,0:T(8,128)S(1)}, f32[16,22,3]{2,1,0:T(8,128)S(1)}, u32[]{:S(2)}, u32[]{:S(2)}) collective-permute-start(f32[16,22,3]{2,1,0:T(8,128)S(1)} %get-tuple-element.84), channel_id=1, source_target_pairs={{0,1},{1,2},{2,3},{4,5},{5,6},{6,7},{8,9},{9,10},{10,11},{12,13},{... | collective-permute-start | bytes 12680 | tf_op jit(solution)/shard_map/ppermute | solution.py:30
  206.1 10.6 %collective-permute-start.56 = (f32[1026]{0:T(1024)S(1)}, f32[1026]{0:T(1024)S(1)}, u32[]{:S(2)}, u32[]{:S(2)}) collective-permute-start(f32[1026]{0:T(1024)S(1)} %concatenate.88), channel_id=1, source_target_pairs={{0,8},{4,12},{8,0},{12,4},{1,9},{5,13},{9,1},{13,5},{2,10},{6,14},... | collective-permute-start | bytes 12320 | tf_op jit(solution)/shard_map/ppermute | solution.py:185
  218.4 10.9 %collective-permute-start.61 = (f32[1026]{0:T(1024)S(1)}, f32[1026]{0:T(1024)S(1)}, u32[]{:S(2)}, u32[]{:S(2)}) collective-permute-start(f32[1026]{0:T(1024)S(1)} %add_add_fusion.1), channel_id=1, source_target_pairs={{0,2},{1,3},{2,0},{3,1},{4,6},{5,7},{6,4},{7,5},{8,10},{9,11},{10,... | collective-permute-start | bytes 12320 | tf_op jit(solution)/shard_map/ppermute | solution.py:185
  221.0 8.3 %collective-permute-start.62 = (f32[1026]{0:T(1024)S(1)}, f32[1026]{0:T(1024)S(1)}, u32[]{:S(2)}, u32[]{:S(2)}) collective-permute-start(f32[1026]{0:T(1024)S(1)} %add_add_fusion.1), channel_id=1, source_target_pairs={{0,3},{1,2},{2,1},{3,0},{4,7},{5,6},{6,5},{7,4},{8,11},{9,10},{10,... | collective-permute-start | bytes 12320 | tf_op jit(solution)/shard_map/ppermute | solution.py:185
  223.4 7.6 %collective-permute-start.59 = (f32[16,22,3]{2,1,0:T(8,128)S(1)}, f32[16,22,3]{2,1,0:T(8,128)S(1)}, u32[]{:S(2)}, u32[]{:S(2)}) collective-permute-start(f32[16,22,3]{2,1,0:T(8,128)S(1)} %get-tuple-element.83), channel_id=1, source_target_pairs={{1,0},{2,1},{3,2},{5,4},{6,5},{7,6},{9,8},{10,9},{11,10},{13,12},{... | collective-permute-start | bytes 12680 | tf_op jit(solution)/shard_map/ppermute | solution.py:31
  224.7 7.7 %collective-permute-start.58 = (f32[16,22,3]{2,1,0:T(8,128)S(1)}, f32[16,22,3]{2,1,0:T(8,128)S(1)}, u32[]{:S(2)}, u32[]{:S(2)}) collective-permute-start(f32[16,22,3]{2,1,0:T(8,128)S(1)} %get-tuple-element.82), channel_id=1, source_target_pairs={{0,1},{1,2},{2,3},{4,5},{5,6},{6,7},{8,9},{9,10},{10,11},{12,13},{... | collective-permute-start | bytes 12680 | tf_op jit(solution)/shard_map/ppermute | solution.py:30
  (85 other events, 377.4 us)
